TPU v7x, 32 devices: a whole 2x2x4 slice. The times are simulated.
32 devices in a mesh: seq: 16 (over z, y, core), fsdp: 2 (over x).
Axes of the slice: x: 2, y: 2, z: 4, core: 2. Of those that a mesh axis runs over, the one named last changes fastest.
Arguments:
- queries: bfloat16 [2, 8192, 1024], P('fsdp', 'seq'), may hold values from -10.5 to 10.5
- key_vectors: bfloat16 [2, 8192, 1024], P('fsdp', 'seq'), may hold values from -10.5 to 10.5
- value_vectors: bfloat16 [2, 8192, 1024], P('fsdp', 'seq'), may hold values from -6 to 6
- grad_mixed: bfloat16 [2, 8192, 2048], P('fsdp', 'seq'), may hold values from -24 to 24
- out_weight: bfloat16 [1024, 2048], P('fsdp'), may hold values from -0.1875 to 0.1875
- head_phase: int32 [8], replicated, may hold values from 0 to 3
- segments_short: int32 [7], replicated, may hold values from 1 to 2048, 8192 in all
- segments_long: int32 [1], replicated, may hold values from 1 to 8192, as said below
Outputs:
- grad_query: bfloat16 [2, 8192, 1024], P('fsdp', 'seq')
- grad_key: bfloat16 [2, 8192, 1024], P('fsdp', 'seq')
- grad_value: bfloat16 [2, 8192, 1024], P('fsdp', 'seq')
Inputs may be any that keep to these rules, and one draw needn't show every extreme that they name: `segments_long`: lengths that sum to 8192; the last of them is 8192, the others are shorter.
All inputs are finite; a program needn't handle non-finite values.
Results may differ from a plain program's by a relative error of at most 0.0095.
Values may be sent and summed in bfloat16 or wider, within the bound.
No kernel may reach another device: no remote copies, remote signals or barrier semaphores. Data moves between devices by JAX's collectives and lax.ppermute only.
A program may use at most 256 MiB of HBM per device.

v0:
```python
import math

import jax
import jax.numpy as jnp
from jax import lax
from jax.sharding import PartitionSpec as P

REACH_SHORT = 4
REACH_LONG = 16


VERY_NEGATIVE = -1e30


def passed_along(value, axis, by):
    devices = lax.axis_size(axis)
    pairs = [(i, i + by) for i in range(devices) if 0 <= i + by < devices]
    return lax.ppermute(value, axis, pairs)


def take_half(tensor, parity):
    layout = tensor.shape
    paired = tensor.reshape(layout[:-3] + (layout[-3] // 2, 2) + layout[-2:])
    return jnp.where((parity == 0)[:, None], paired[..., 0, :, :], paired[..., 1, :, :])


def put_half(tensor, parity):
    zero_fill = jnp.zeros_like(tensor)
    first_half = jnp.where((parity == 0)[:, None], tensor, zero_fill)
    second_half = jnp.where((parity == 1)[:, None], tensor, zero_fill)
    stacked = jnp.stack([first_half, second_half], axis=-3)
    return stacked.reshape(tensor.shape[:-3] + (2 * tensor.shape[-3],) + tensor.shape[-2:])


def stat_half(tensor, parity):
    paired = tensor.reshape(tensor.shape[0], tensor.shape[1] // 2, 2)
    return jnp.where((parity == 0)[:, None], paired[:, :, 0], paired[:, :, 1])


def stat_put(tensor, parity, fill_value):
    filler = jnp.full_like(tensor, fill_value)
    first_half = jnp.where((parity == 0)[:, None], tensor, filler)
    second_half = jnp.where((parity == 1)[:, None], tensor, filler)
    return jnp.stack([first_half, second_half], axis=-1).reshape(
        tensor.shape[0], 2 * tensor.shape[1]
    )


def segment_of(positions, lengths):
    seg_ends = jnp.cumsum(lengths)
    return jnp.sum((positions[..., None] >= seg_ends).astype(jnp.int32), axis=-1)


def row_positions(shard_index, tok_dev, stride, offset, row_count):
    return (
        shard_index * tok_dev
        + stride * jnp.arange(row_count, dtype=jnp.int32)[None, :]
        + offset[:, None]
    )


def pair_mask(query_pos, key_pos, lengths):
    query_seg = segment_of(query_pos, lengths)
    key_seg = segment_of(key_pos, lengths)
    causal = key_pos[:, None, :] <= query_pos[:, :, None]
    same_seg = key_seg[:, None, :] == query_seg[:, :, None]
    return causal & same_seg & (key_pos[:, None, :] >= 0)


def product(pattern, left_operand, right_operand):
    return jnp.einsum(pattern, left_operand, right_operand, preferred_element_type=jnp.float32)


def guarded(is_live, compute, shapes):
    return compute()


def shard_grads(
    shard_index,
    query_rows,
    grad_rows,
    near_window,
    far_window,
    head_phase,
    segments_short,
    segments_long,
    guard_fn,
    product_fn,
):
    rows_short, head_count, head_width = query_rows.shape
    tok_dev = 2 * rows_short
    score_scale = 1.0 / math.sqrt(head_width)
    par_short = head_phase % 2
    par_long = head_phase // 2
    query_long = take_half(query_rows, par_long)
    grad_long = take_half(grad_rows, par_long)
    levels = [
        (query_rows, grad_rows, near_window, 2, par_short, segments_short),
        (query_long, grad_long, far_window, 4, head_phase, segments_long),
    ]
    stored = []
    peak_list = []
    for query_here, grad_here, window, stride, offset, lengths in levels:
        row_count = query_here.shape[0]
        query_pos = row_positions(shard_index, tok_dev, stride, offset, row_count)
        blocks = []
        top_here = jnp.full((head_count, row_count), VERY_NEGATIVE, jnp.float32)
        for distance in range(len(window)):
            key_pos = row_positions(shard_index - distance, tok_dev, stride, offset, row_count)
            live_pairs = pair_mask(query_pos, key_pos, lengths)

            def score_block(query_here=query_here, key_here=window[distance][0]):
                return (product_fn("qhd,khd->hqk", query_here, key_here) * score_scale,)

            raw_scores = guard_fn(
                jnp.any(live_pairs), score_block, ((head_count, row_count, row_count),)
            )[0]
            scores = jnp.where(live_pairs, raw_scores, VERY_NEGATIVE)
            top_here = jnp.maximum(top_here, jnp.max(scores, axis=-1))
            blocks.append((live_pairs, scores))
        stored.append(blocks)
        peak_list.append(top_here)
    top_short = jnp.maximum(peak_list[0], stat_put(peak_list[1], par_long, VERY_NEGATIVE))
    level_tops = [top_short, stat_half(top_short, par_long)]
    totals = []
    numerators = []
    for level_index, (query_here, grad_here, window, stride, offset, lengths) in enumerate(levels):
        row_count = query_here.shape[0]
        total_here = jnp.zeros((head_count, row_count), jnp.float32)
        numer_here = jnp.zeros((row_count, head_count, head_width), jnp.float32)
        for distance, (live_pairs, scores) in enumerate(stored[level_index]):
            weights = jnp.where(
                live_pairs, jnp.exp(scores - level_tops[level_index][:, :, None]), 0.0
            )
            total_here = total_here + jnp.sum(weights, axis=-1)

            def weight_block(weights=weights, value_here=window[distance][1]):
                return (product_fn("hqk,khd->qhd", weights.astype(jnp.bfloat16), value_here),)

            numer_here = (
                numer_here
                + guard_fn(
                    jnp.any(live_pairs), weight_block, ((row_count, head_count, head_width),)
                )[0]
            )
        totals.append(total_here)
        numerators.append(numer_here)
    denominator = totals[0] + stat_put(totals[1], par_long, 0.0)
    attended = (numerators[0] + put_half(numerators[1], par_long)) / jnp.transpose(denominator)[
        :, :, None
    ]
    delta_rows = jnp.transpose(jnp.sum(grad_rows.astype(jnp.float32) * attended, axis=-1))
    inverse = 1.0 / denominator
    level_inverse = [inverse, stat_half(inverse, par_long)]
    level_delta = [delta_rows, stat_half(delta_rows, par_long)]
    grad_levels = []
    part_levels = []
    for level_index, (query_here, grad_here, window, stride, offset, lengths) in enumerate(levels):
        row_count = query_here.shape[0]
        grad_sum = jnp.zeros((row_count, head_count, head_width), jnp.float32)
        part_list = []
        for distance, (live_pairs, scores) in enumerate(stored[level_index]):

            def backward_block(
                live_pairs=live_pairs,
                scores=scores,
                key_here=window[distance][0],
                value_here=window[distance][1],
                query_here=query_here,
                grad_here=grad_here,
                top_here=level_tops[level_index],
                inverse_here=level_inverse[level_index],
                delta_here=level_delta[level_index],
            ):
                probability = (
                    jnp.where(live_pairs, jnp.exp(scores - top_here[:, :, None]), 0.0)
                    * inverse_here[:, :, None]
                )
                grad_probs = product_fn("qhd,khd->hqk", grad_here, value_here)
                grad_scores = (probability * (grad_probs - delta_here[:, :, None])).astype(
                    jnp.bfloat16
                )
                return (
                    product_fn("hqk,khd->qhd", grad_scores, key_here) * score_scale,
                    product_fn("hqk,qhd->khd", grad_scores, query_here) * score_scale,
                    product_fn("hqk,qhd->khd", probability.astype(jnp.bfloat16), grad_here),
                )

            shapes = ((row_count, head_count, head_width),) * 3
            add_query, part_key, part_value = guard_fn(jnp.any(live_pairs), backward_block, shapes)
            grad_sum = grad_sum + add_query
            part_list.append((part_key, part_value))
        grad_levels.append(grad_sum)
        part_levels.append(part_list)
    grad_query = grad_levels[0] + put_half(grad_levels[1], par_long)
    near_parts = []
    for distance in range(len(near_window)):
        key_part = part_levels[0][distance][0] + put_half(part_levels[1][distance][0], par_long)
        value_part = part_levels[0][distance][1] + put_half(part_levels[1][distance][1], par_long)
        near_parts.append(jnp.stack([key_part, value_part]).astype(jnp.bfloat16))
    far_parts = [
        jnp.stack([part_levels[1][distance][0], part_levels[1][distance][1]]).astype(jnp.bfloat16)
        for distance in range(len(near_window), len(far_window))
    ]
    return (grad_query, near_parts, far_parts, (top_short, inverse, delta_rows))


def shards(
    queries,
    key_vectors,
    value_vectors,
    grad_mixed,
    out_weight,
    head_phase,
    segments_short,
    segments_long,
):
    shard_index = lax.axis_index("seq")
    tok_dev = queries.shape[1]
    head_count = head_phase.shape[0]
    head_width = queries.shape[2] // head_count
    par_short = head_phase % 2
    par_long = head_phase // 2
    grad_out = jnp.einsum(
        "td,rd->tr",
        grad_mixed[0],
        lax.all_gather(out_weight, "fsdp", axis=0, tiled=True),
        preferred_element_type=jnp.float32,
    ).astype(jnp.bfloat16)

    def split_rows(tensor):
        return take_half(tensor.reshape(tok_dev, head_count, head_width), par_short)

    query_rows = split_rows(queries[0])
    grad_rows = split_rows(grad_out)
    own_short = jnp.stack([split_rows(key_vectors[0]), split_rows(value_vectors[0])])
    own_long = take_half(own_short, par_long)
    near_window = [own_short]
    far_window = [own_long]
    for distance in range(1, REACH_SHORT + 1):
        arrived = passed_along(own_short, "seq", distance)
        near_window.append(arrived)
        far_window.append(take_half(arrived, par_long))
    for distance in range(REACH_SHORT + 1, REACH_LONG + 1):
        far_window.append(passed_along(own_long, "seq", distance))
    grad_query, near_parts, far_parts, row_stats = shard_grads(
        shard_index,
        query_rows,
        grad_rows,
        near_window,
        far_window,
        head_phase,
        segments_short,
        segments_long,
        guarded,
        product,
    )
    summed = near_parts[0].astype(jnp.float32)
    far_sum = jnp.zeros(own_long.shape, jnp.float32)
    for distance in range(1, REACH_SHORT + 1):
        summed = summed + passed_along(near_parts[distance], "seq", -distance).astype(jnp.float32)
    for distance in range(REACH_SHORT + 1, REACH_LONG + 1):
        far_sum = far_sum + passed_along(
            far_parts[distance - REACH_SHORT - 1], "seq", -distance
        ).astype(jnp.float32)
    summed = summed + put_half(far_sum, par_long)
    final_pair = summed.astype(jnp.bfloat16)

    def to_tokens(rows_here):
        return put_half(rows_here, par_short).reshape(1, tok_dev, head_count * head_width)

    return (
        to_tokens(grad_query.astype(jnp.bfloat16)),
        to_tokens(final_pair[0]),
        to_tokens(final_pair[1]),
    )


def solution(mesh):
    placed = (
        P("fsdp", "seq", None),
        P("fsdp", "seq", None),
        P("fsdp", "seq", None),
        P("fsdp", "seq", None),
        P("fsdp", None),
        P(),
        P(),
        P(),
    )
    return jax.shard_map(
        shards,
        mesh=mesh,
        in_specs=placed,
        out_specs=(P("fsdp", "seq", None), P("fsdp", "seq", None), P("fsdp", "seq", None)),
        check_vma=False,
    )
```

profile of v0, /device:TPU:5, one launch (start us, length us, event | category | flops | bytes accessed | tf_op | source)
XLA Modules:
  0.0 676.5 jit_solution(2493510021028953090)
XLA Ops:
  12.9 3.3 collective-permute-start.3
  16.2 4.0 collective-permute-start.2
  20.2 3.1 collective-permute-start.1
  23.3 2.8 collective-permute-start
  38.3 57.3 %collective-permute-done = bf16[2,256,8,128]{3,1,2,0:T(8,128)(2,1)} collective-permute-done((bf16[2,256,8,128]{3,1,2,0:T(8,128)(2,1)}, bf16[2,256,8,128]{3,1,2,0:T(8,128)(2,1)}, u32[]{:S(2)}, u32[]{:S(2)}) %collective-permute-start) | collective-permute-done | bytes 1048608 | tf_op jit(solution)/shard_map/ppermute | solution.py:18
  95.6 3.6 fusion.323
  99.2 3.7 fusion.324
  102.9 3.7 fusion.325
  116.2 2.6 collective-permute-start.11
  118.8 4.5 fusion.10
  126.4 2.3 fusion.348
  142.0 6.5 collective-permute-start.8
  165.5 7.0 %collective-permute-done.7 = bf16[2,128,8,128]{3,1,2,0:T(8,128)(2,1)S(1)} collective-permute-done((bf16[2,128,8,128]{3,1,2,0:T(8,128)(2,1)}, bf16[2,128,8,128]{3,1,2,0:T(8,128)(2,1)S(1)}, u32[]{:S(2)}, u32[]{:S(2)}) %collective-permute-start.7) | collective-permute-done | bytes 524320 | tf_op jit(solution)/shard_map/ppermute | solution.py:18
  174.4 9.3 %collective-permute-done.6 = bf16[2,128,8,128]{3,1,2,0:T(8,128)(2,1)S(1)} collective-permute-done((bf16[2,128,8,128]{3,1,2,0:T(8,128)(2,1)}, bf16[2,128,8,128]{3,1,2,0:T(8,128)(2,1)S(1)}, u32[]{:S(2)}, u32[]{:S(2)}) %collective-permute-start.6) | collective-permute-done | bytes 524320 | tf_op jit(solution)/shard_map/ppermute | solution.py:18
  185.7 9.2 %collective-permute-done.5 = bf16[2,128,8,128]{3,1,2,0:T(8,128)(2,1)S(1)} collective-permute-done((bf16[2,128,8,128]{3,1,2,0:T(8,128)(2,1)}, bf16[2,128,8,128]{3,1,2,0:T(8,128)(2,1)S(1)}, u32[]{:S(2)}, u32[]{:S(2)}) %collective-permute-start.5) | collective-permute-done | bytes 524320 | tf_op jit(solution)/shard_map/ppermute | solution.py:18
  198.9 7.2 %collective-permute-done.4 = bf16[2,128,8,128]{3,1,2,0:T(8,128)(2,1)S(1)} collective-permute-done((bf16[2,128,8,128]{3,1,2,0:T(8,128)(2,1)}, bf16[2,128,8,128]{3,1,2,0:T(8,128)(2,1)S(1)}, u32[]{:S(2)}, u32[]{:S(2)}) %collective-permute-start.4) | collective-permute-done | bytes 524320 | tf_op jit(solution)/shard_map/ppermute | solution.py:18
  213.2 5.9 fusion.2
  219.1 3.0 fusion.3
  226.0 5.0 fusion.296
  231.1 5.1 fusion.299
  236.3 4.9 fusion.302
  245.6 7.4 %fusion.318 = (f32[8,256]{1,0:T(8,128)S(1)}, f32[8,256]{1,0:T(8,128)S(1)}, f32[8,256]{1,0:T(8,128)S(1)}, f32[8,256]{1,0:T(8,128)S(1)}) fusion(f32[8,256]{1,0:T(8,128)S(1)} %get-tuple-element.40, f32[8,256,256]{1,2,0:T(8,128)} %get-tuple-element.262, pred[8,256]{1,0:T(8,128)(4,1)} %get-tuple-element.152, s32[8,256]{1,0:T(8,128)S(1)} %get-tuple-element.31, ...), kind=kLoop, calls=%fused_computation.707 | loop fusion | flops 18866176 | bytes 8503296 | tf_op jit(solution)/shard_map/reduce_sum | solution.py:135
  253.7 2.7 fusion.252
  256.4 4.5 fusion.180
  295.4 3.8 fusion.176
  299.2 4.0 fusion.174
  303.2 3.8 convolution_add_fusion.3
  307.1 3.4 fusion.50
  339.7 2.4 multiply_convert_fusion.4
  382.9 2.7 fusion.59
  388.1 2.6 fusion.58
  393.2 2.5 fusion.57
  398.3 2.3 multiply_convert_fusion.3
  401.0 2.4 multiply_convert_fusion.2
  403.8 2.4 multiply_convert_fusion.1
  408.4 2.6 multiply_convert_fusion
  422.4 2.6 fusion.56
  434.5 56.6 %collective-permute-done.27 = bf16[2,128,8,128]{3,1,2,0:T(8,128)(2,1)S(1)} collective-permute-done((bf16[2,128,8,128]{3,1,2,0:T(8,128)(2,1)S(1)}, bf16[2,128,8,128]{3,1,2,0:T(8,128)(2,1)S(1)}, u32[]{:S(2)}, u32[]{:S(2)}) %collective-permute-start.27) | collective-permute-done | bytes 524320 | tf_op jit(solution)/shard_map/ppermute | solution.py:18
  499.6 4.8 collective-permute-done.26
  505.8 2.7 fusion.60
  510.2 10.8 %collective-permute-done.24 = bf16[2,128,8,128]{3,1,2,0:T(8,128)(2,1)} collective-permute-done((bf16[2,128,8,128]{3,1,2,0:T(8,128)(2,1)}, bf16[2,128,8,128]{3,1,2,0:T(8,128)(2,1)}, u32[]{:S(2)}, u32[]{:S(2)}) %collective-permute-start.24) | collective-permute-done | bytes 524320 | tf_op jit(solution)/shard_map/ppermute | solution.py:18
  521.0 40.5 %collective-permute-start.18 = (bf16[2,256,8,128]{3,1,2,0:T(8,128)(2,1)S(1)}, bf16[2,256,8,128]{3,1,2,0:T(8,128)(2,1)S(1)}, u32[]{:S(2)}, u32[]{:S(2)}) collective-permute-start(bf16[2,256,8,128]{3,1,2,0:T(8,128)(2,1)S(1)} %copy-done.52), channel_id=1, source_target_pairs={{6,0},{8,2},{10,4},{12,6},{14,8},{16,10},{18,12},{20,14},{22,16},{... | collective-permute-start | bytes 3145736 | tf_op jit(solution)/shard_map/ppermute | solution.py:18
  561.5 16.9 %collective-permute-done.23 = bf16[2,128,8,128]{3,1,2,0:T(8,128)(2,1)} collective-permute-done((bf16[2,128,8,128]{3,1,2,0:T(8,128)(2,1)}, bf16[2,128,8,128]{3,1,2,0:T(8,128)(2,1)}, u32[]{:S(2)}, u32[]{:S(2)}) %collective-permute-start.23) | collective-permute-done | bytes 524320 | tf_op jit(solution)/shard_map/ppermute | solution.py:18
  580.3 7.2 %collective-permute-done.22 = bf16[2,128,8,128]{3,1,2,0:T(8,128)(2,1)} collective-permute-done((bf16[2,128,8,128]{3,1,2,0:T(8,128)(2,1)}, bf16[2,128,8,128]{3,1,2,0:T(8,128)(2,1)}, u32[]{:S(2)}, u32[]{:S(2)}) %collective-permute-start.22) | collective-permute-done | bytes 524320 | tf_op jit(solution)/shard_map/ppermute | solution.py:18
  592.4 2.8 select_bitcast_fusion.1
  597.2 12.4 %collective-permute-done.18 = bf16[2,256,8,128]{3,1,2,0:T(8,128)(2,1)S(1)} collective-permute-done((bf16[2,256,8,128]{3,1,2,0:T(8,128)(2,1)S(1)}, bf16[2,256,8,128]{3,1,2,0:T(8,128)(2,1)S(1)}, u32[]{:S(2)}, u32[]{:S(2)}) %collective-permute-start.18) | collective-permute-done | bytes 1048608 | tf_op jit(solution)/shard_map/ppermute | solution.py:18
  609.6 39.1 %collective-permute-done.17 = bf16[2,256,8,128]{3,1,2,0:T(8,128)(2,1)S(1)} collective-permute-done((bf16[2,256,8,128]{3,1,2,0:T(8,128)(2,1)S(1)}, bf16[2,256,8,128]{3,1,2,0:T(8,128)(2,1)S(1)}, u32[]{:S(2)}, u32[]{:S(2)}) %collective-permute-start.17) | collective-permute-done | bytes 1048608 | tf_op jit(solution)/shard_map/ppermute | solution.py:18
  648.6 11.0 %collective-permute-done.16 = bf16[2,256,8,128]{3,1,2,0:T(8,128)(2,1)S(1)} collective-permute-done((bf16[2,256,8,128]{3,1,2,0:T(8,128)(2,1)S(1)}, bf16[2,256,8,128]{3,1,2,0:T(8,128)(2,1)S(1)}, u32[]{:S(2)}, u32[]{:S(2)}) %collective-permute-start.16) | collective-permute-done | bytes 1048608 | tf_op jit(solution)/shard_map/ppermute | solution.py:18
  (711 shorter events, 245.8 us)
Async XLA Ops:
  7.2 111.6 %all-gather.2.cloned.1.call-start = ((), (), s32[]{:S(2)}) async-start(), calls=%async_computation | async-start | bytes 6291456 | tf_op jit(solution)/shard_map/all_gather | solution.py:227
  8.7 283.4 %copy-start.124 = (pred[8]{0:T(512)(128)(4,1)}, pred[8]{0:T(512)(128)(4,1)S(1)}, u32[]{:S(2)}) copy-start(pred[8]{0:T(512)(128)(4,1)S(1)} %get-tuple-element.44) | copy-start | bytes 28
  12.9 93.8 %collective-permute-start.3 = (bf16[2,256,8,128]{3,1,2,0:T(8,128)(2,1)}, bf16[2,256,8,128]{3,1,2,0:T(8,128)(2,1)S(1)}, u32[]{:S(2)}, u32[]{:S(2)}) collective-permute-start(bf16[2,256,8,128]{3,1,2,0:T(8,128)(2,1)} %pad_maximum_fusion.1), channel_id=1, source_target_pairs={{0,8},{2,10},{4,12},{6,14},{8,16},{10,18},{12,20},{14,22},{16,24},... | collective-permute-start | bytes 3145736 | tf_op jit(solution)/shard_map/ppermute | solution.py:18
  16.2 86.8 %collective-permute-start.2 = (bf16[2,256,8,128]{3,1,2,0:T(8,128)(2,1)}, bf16[2,256,8,128]{3,1,2,0:T(8,128)(2,1)}, u32[]{:S(2)}, u32[]{:S(2)}) collective-permute-start(bf16[2,256,8,128]{3,1,2,0:T(8,128)(2,1)} %pad_maximum_fusion.1), channel_id=1, source_target_pairs={{0,6},{2,8},{4,10},{6,12},{8,14},{10,16},{12,18},{14,20},{16,22},{... | collective-permute-start | bytes 3145736 | tf_op jit(solution)/shard_map/ppermute | solution.py:18
  20.2 79.1 %collective-permute-start.1 = (bf16[2,256,8,128]{3,1,2,0:T(8,128)(2,1)}, bf16[2,256,8,128]{3,1,2,0:T(8,128)(2,1)}, u32[]{:S(2)}, u32[]{:S(2)}) collective-permute-start(bf16[2,256,8,128]{3,1,2,0:T(8,128)(2,1)} %pad_maximum_fusion.1), channel_id=1, source_target_pairs={{0,4},{2,6},{4,8},{6,10},{8,12},{10,14},{12,16},{14,18},{16,20},{1... | collective-permute-start | bytes 3145736 | tf_op jit(solution)/shard_map/ppermute | solution.py:18
  23.3 72.2 %collective-permute-start = (bf16[2,256,8,128]{3,1,2,0:T(8,128)(2,1)}, bf16[2,256,8,128]{3,1,2,0:T(8,128)(2,1)}, u32[]{:S(2)}, u32[]{:S(2)}) collective-permute-start(bf16[2,256,8,128]{3,1,2,0:T(8,128)(2,1)} %pad_maximum_fusion.1), channel_id=1, source_target_pairs={{0,2},{2,4},{4,6},{6,8},{8,10},{10,12},{12,14},{14,16},{16,18},{18... | collective-permute-start | bytes 3145736 | tf_op jit(solution)/shard_map/ppermute | solution.py:18
  26.5 246.8 %copy-start.126 = (s32[8,128]{1,0:T(8,128)}, s32[8,128]{1,0:T(8,128)S(1)}, u32[]{:S(2)}) copy-start(s32[8,128]{1,0:T(8,128)S(1)} %get-tuple-element.207) | copy-start | bytes 12292
  26.5 248.3 %copy-start.142 = (s32[8,128]{1,0:T(8,128)}, s32[8,128]{1,0:T(8,128)S(1)}, u32[]{:S(2)}) copy-start(s32[8,128]{1,0:T(8,128)S(1)} %get-tuple-element.206) | copy-start | bytes 12292
  26.5 250.6 %copy-start.144 = (s32[8,128]{1,0:T(8,128)}, s32[8,128]{1,0:T(8,128)S(1)}, u32[]{:S(2)}) copy-start(s32[8,128]{1,0:T(8,128)S(1)} %get-tuple-element.205) | copy-start | bytes 12292
  26.5 252.8 %copy-start.148 = (s32[8,128]{1,0:T(8,128)}, s32[8,128]{1,0:T(8,128)S(1)}, u32[]{:S(2)}) copy-start(s32[8,128]{1,0:T(8,128)S(1)} %get-tuple-element.204) | copy-start | bytes 12292
  26.6 255.0 %copy-start.150 = (s32[8,128]{1,0:T(8,128)}, s32[8,128]{1,0:T(8,128)S(1)}, u32[]{:S(2)}) copy-start(s32[8,128]{1,0:T(8,128)S(1)} %get-tuple-element.203) | copy-start | bytes 12292
  26.6 257.3 %copy-start.130 = (s32[8,128]{1,0:T(8,128)}, s32[8,128]{1,0:T(8,128)S(1)}, u32[]{:S(2)}) copy-start(s32[8,128]{1,0:T(8,128)S(1)} %get-tuple-element.213) | copy-start | bytes 12292
  26.6 259.3 %copy-start.132 = (s32[8,128]{1,0:T(8,128)}, s32[8,128]{1,0:T(8,128)S(1)}, u32[]{:S(2)}) copy-start(s32[8,128]{1,0:T(8,128)S(1)} %get-tuple-element.212) | copy-start | bytes 12292
  26.6 261.4 %copy-start.134 = (s32[8,128]{1,0:T(8,128)}, s32[8,128]{1,0:T(8,128)S(1)}, u32[]{:S(2)}) copy-start(s32[8,128]{1,0:T(8,128)S(1)} %get-tuple-element.211) | copy-start | bytes 12292
  26.6 263.5 %copy-start.136 = (s32[8,128]{1,0:T(8,128)}, s32[8,128]{1,0:T(8,128)S(1)}, u32[]{:S(2)}) copy-start(s32[8,128]{1,0:T(8,128)S(1)} %get-tuple-element.210) | copy-start | bytes 12292
  35.3 267.9 %copy-start.120 = (s32[8,256]{1,0:T(8,128)}, s32[8,256]{1,0:T(8,128)S(1)}, u32[]{:S(2)}) copy-start(s32[8,256]{1,0:T(8,128)S(1)} %get-tuple-element.27) | copy-start | bytes 24580
  36.3 247.6 %copy-start.146 = (s32[8,128]{1,0:T(8,128)}, s32[8,128]{1,0:T(8,128)S(1)}, u32[]{:S(2)}) copy-start(s32[8,128]{1,0:T(8,128)S(1)} %get-tuple-element.162) | copy-start | bytes 12292
  36.3 249.6 %copy-start.152 = (s32[8,128]{1,0:T(8,128)}, s32[8,128]{1,0:T(8,128)S(1)}, u32[]{:S(2)}) copy-start(s32[8,128]{1,0:T(8,128)S(1)} %get-tuple-element.164) | copy-start | bytes 12292
  36.3 251.8 %copy-start.154 = (s32[8,128]{1,0:T(8,128)}, s32[8,128]{1,0:T(8,128)S(1)}, u32[]{:S(2)}) copy-start(s32[8,128]{1,0:T(8,128)S(1)} %get-tuple-element.166) | copy-start | bytes 12292
  36.3 253.8 %copy-start.156 = (s32[8,128]{1,0:T(8,128)}, s32[8,128]{1,0:T(8,128)S(1)}, u32[]{:S(2)}) copy-start(s32[8,128]{1,0:T(8,128)S(1)} %get-tuple-element.168) | copy-start | bytes 12292
  110.4 24.4 %collective-permute-start.15 = (bf16[2,128,8,128]{3,1,2,0:T(8,128)(2,1)}, bf16[2,128,8,128]{3,1,2,0:T(8,128)(2,1)}, u32[]{:S(2)}, u32[]{:S(2)}) collective-permute-start(bf16[2,128,8,128]{3,1,2,0:T(8,128)(2,1)} %get-tuple-element.198), channel_id=1, source_target_pairs={} | collective-permute-start | bytes 1572872 | tf_op jit(solution)/shard_map/ppermute | solution.py:18
  111.8 26.6 %collective-permute-start.14 = (bf16[2,128,8,128]{3,1,2,0:T(8,128)(2,1)}, bf16[2,128,8,128]{3,1,2,0:T(8,128)(2,1)}, u32[]{:S(2)}, u32[]{:S(2)}) collective-permute-start(bf16[2,128,8,128]{3,1,2,0:T(8,128)(2,1)} %get-tuple-element.198), channel_id=1, source_target_pairs={{0,30},{1,31}} | collective-permute-start | bytes 1572872 | tf_op jit(solution)/shard_map/ppermute | solution.py:18
  113.3 28.7 %collective-permute-start.13 = (bf16[2,128,8,128]{3,1,2,0:T(8,128)(2,1)}, bf16[2,128,8,128]{3,1,2,0:T(8,128)(2,1)}, u32[]{:S(2)}, u32[]{:S(2)}) collective-permute-start(bf16[2,128,8,128]{3,1,2,0:T(8,128)(2,1)} %get-tuple-element.198), channel_id=1, source_target_pairs={{0,28},{2,30},{1,29},{3,31}} | collective-permute-start | bytes 1572872 | tf_op jit(solution)/shard_map/ppermute | solution.py:18
  114.7 36.1 %collective-permute-start.12 = (bf16[2,128,8,128]{3,1,2,0:T(8,128)(2,1)}, bf16[2,128,8,128]{3,1,2,0:T(8,128)(2,1)}, u32[]{:S(2)}, u32[]{:S(2)}) collective-permute-start(bf16[2,128,8,128]{3,1,2,0:T(8,128)(2,1)} %get-tuple-element.198), channel_id=1, source_target_pairs={{0,26},{2,28},{4,30},{1,27},{3,29},{5,31}} | collective-permute-start | bytes 1572872 | tf_op jit(solution)/shard_map/ppermute | solution.py:18
  116.2 38.2 %collective-permute-start.11 = (bf16[2,128,8,128]{3,1,2,0:T(8,128)(2,1)}, bf16[2,128,8,128]{3,1,2,0:T(8,128)(2,1)}, u32[]{:S(2)}, u32[]{:S(2)}) collective-permute-start(bf16[2,128,8,128]{3,1,2,0:T(8,128)(2,1)} %get-tuple-element.198), channel_id=1, source_target_pairs={{0,24},{2,26},{4,28},{6,30},{1,25},{3,27},{5,29},{7,31}} | collective-permute-start | bytes 1572872 | tf_op jit(solution)/shard_map/ppermute | solution.py:18
  134.8 23.2 %collective-permute-start.10 = (bf16[2,128,8,128]{3,1,2,0:T(8,128)(2,1)}, bf16[2,128,8,128]{3,1,2,0:T(8,128)(2,1)S(1)}, u32[]{:S(2)}, u32[]{:S(2)}) collective-permute-start(bf16[2,128,8,128]{3,1,2,0:T(8,128)(2,1)} %get-tuple-element.198), channel_id=1, source_target_pairs={{0,22},{2,24},{4,26},{6,28},{8,30},{1,23},{3,25},{5,27},{7,29},{9,... | collective-permute-start | bytes 1572872 | tf_op jit(solution)/shard_map/ppermute | solution.py:18
  138.4 22.2 %collective-permute-start.9 = (bf16[2,128,8,128]{3,1,2,0:T(8,128)(2,1)}, bf16[2,128,8,128]{3,1,2,0:T(8,128)(2,1)S(1)}, u32[]{:S(2)}, u32[]{:S(2)}) collective-permute-start(bf16[2,128,8,128]{3,1,2,0:T(8,128)(2,1)} %get-tuple-element.198), channel_id=1, source_target_pairs={{0,20},{2,22},{4,24},{6,26},{8,28},{10,30},{1,21},{3,23},{5,25},{7... | collective-permute-start | bytes 1572872 | tf_op jit(solution)/shard_map/ppermute | solution.py:18
  142.0 21.5 %collective-permute-start.8 = (bf16[2,128,8,128]{3,1,2,0:T(8,128)(2,1)}, bf16[2,128,8,128]{3,1,2,0:T(8,128)(2,1)S(1)}, u32[]{:S(2)}, u32[]{:S(2)}) collective-permute-start(bf16[2,128,8,128]{3,1,2,0:T(8,128)(2,1)} %get-tuple-element.198), channel_id=1, source_target_pairs={{0,18},{2,20},{4,22},{6,24},{8,26},{10,28},{12,30},{1,19},{3,21},{... | collective-permute-start | bytes 1572872 | tf_op jit(solution)/shard_map/ppermute | solution.py:18
  150.8 21.7 %collective-permute-start.7 = (bf16[2,128,8,128]{3,1,2,0:T(8,128)(2,1)}, bf16[2,128,8,128]{3,1,2,0:T(8,128)(2,1)S(1)}, u32[]{:S(2)}, u32[]{:S(2)}) collective-permute-start(bf16[2,128,8,128]{3,1,2,0:T(8,128)(2,1)} %get-tuple-element.198), channel_id=1, source_target_pairs={{0,16},{2,18},{4,20},{6,22},{8,24},{10,26},{12,28},{14,30},{1,17},... | collective-permute-start | bytes 1572872 | tf_op jit(solution)/shard_map/ppermute | solution.py:18
  154.4 29.3 %collective-permute-start.6 = (bf16[2,128,8,128]{3,1,2,0:T(8,128)(2,1)}, bf16[2,128,8,128]{3,1,2,0:T(8,128)(2,1)S(1)}, u32[]{:S(2)}, u32[]{:S(2)}) collective-permute-start(bf16[2,128,8,128]{3,1,2,0:T(8,128)(2,1)} %get-tuple-element.198), channel_id=1, source_target_pairs={{0,14},{2,16},{4,18},{6,20},{8,22},{10,24},{12,26},{14,28},{16,30}... | collective-permute-start | bytes 1572872 | tf_op jit(solution)/shard_map/ppermute | solution.py:18
  158.0 37.0 %collective-permute-start.5 = (bf16[2,128,8,128]{3,1,2,0:T(8,128)(2,1)}, bf16[2,128,8,128]{3,1,2,0:T(8,128)(2,1)S(1)}, u32[]{:S(2)}, u32[]{:S(2)}) collective-permute-start(bf16[2,128,8,128]{3,1,2,0:T(8,128)(2,1)} %get-tuple-element.198), channel_id=1, source_target_pairs={{0,12},{2,14},{4,16},{6,18},{8,20},{10,22},{12,24},{14,26},{16,28}... | collective-permute-start | bytes 1572872 | tf_op jit(solution)/shard_map/ppermute | solution.py:18
  160.7 45.5 %collective-permute-start.4 = (bf16[2,128,8,128]{3,1,2,0:T(8,128)(2,1)}, bf16[2,128,8,128]{3,1,2,0:T(8,128)(2,1)S(1)}, u32[]{:S(2)}, u32[]{:S(2)}) collective-permute-start(bf16[2,128,8,128]{3,1,2,0:T(8,128)(2,1)} %get-tuple-element.198), channel_id=1, source_target_pairs={{0,10},{2,12},{4,14},{6,16},{8,18},{10,20},{12,22},{14,24},{16,26}... | collective-permute-start | bytes 1572872 | tf_op jit(solution)/shard_map/ppermute | solution.py:18
  374.9 50.1 %collective-permute-start.31 = (bf16[2,128,8,128]{3,1,2,0:T(8,128)(2,1)S(1)}, bf16[2,128,8,128]{3,1,2,0:T(8,128)(2,1)S(1)}, u32[]{:S(2)}, u32[]{:S(2)}) collective-permute-start(bf16[2,128,8,128]{3,1,2,0:T(8,128)(2,1)S(1)} %pad_maximum_fusion.33), channel_id=1, source_target_pairs={} | collective-permute-start | bytes 1572872 | tf_op jit(solution)/shard_map/ppermute | solution.py:18
  375.6 51.5 %collective-permute-start.20 = (bf16[2,128,8,128]{3,1,2,0:T(8,128)(2,1)S(1)}, bf16[2,128,8,128]{3,1,2,0:T(8,128)(2,1)S(1)}, u32[]{:S(2)}, u32[]{:S(2)}) collective-permute-start(bf16[2,128,8,128]{3,1,2,0:T(8,128)(2,1)S(1)} %pad_maximum_fusion.22), channel_id=1, source_target_pairs={{10,0},{12,2},{14,4},{16,6},{18,8},{20,10},{22,12},{24,14},{26,16}... | collective-permute-start | bytes 1572872 | tf_op jit(solution)/shard_map/ppermute | solution.py:18
  377.0 53.6 %collective-permute-start.30 = (bf16[2,128,8,128]{3,1,2,0:T(8,128)(2,1)S(1)}, bf16[2,128,8,128]{3,1,2,0:T(8,128)(2,1)S(1)}, u32[]{:S(2)}, u32[]{:S(2)}) collective-permute-start(bf16[2,128,8,128]{3,1,2,0:T(8,128)(2,1)S(1)} %pad_maximum_fusion.32), channel_id=1, source_target_pairs={{30,0},{31,1}} | collective-permute-start | bytes 1572872 | tf_op jit(solution)/shard_map/ppermute | solution.py:18
  377.8 54.2 %collective-permute-start.29 = (bf16[2,128,8,128]{3,1,2,0:T(8,128)(2,1)S(1)}, bf16[2,128,8,128]{3,1,2,0:T(8,128)(2,1)S(1)}, u32[]{:S(2)}, u32[]{:S(2)}) collective-permute-start(bf16[2,128,8,128]{3,1,2,0:T(8,128)(2,1)S(1)} %pad_maximum_fusion.31), channel_id=1, source_target_pairs={{28,0},{30,2},{29,1},{31,3}} | collective-permute-start | bytes 1572872 | tf_op jit(solution)/shard_map/ppermute | solution.py:18
  378.5 54.7 %collective-permute-start.28 = (bf16[2,128,8,128]{3,1,2,0:T(8,128)(2,1)S(1)}, bf16[2,128,8,128]{3,1,2,0:T(8,128)(2,1)S(1)}, u32[]{:S(2)}, u32[]{:S(2)}) collective-permute-start(bf16[2,128,8,128]{3,1,2,0:T(8,128)(2,1)S(1)} %pad_maximum_fusion.30), channel_id=1, source_target_pairs={{26,0},{28,2},{30,4},{27,1},{29,3},{31,5}} | collective-permute-start | bytes 1572872 | tf_op jit(solution)/shard_map/ppermute | solution.py:18
  425.0 66.2 %collective-permute-start.27 = (bf16[2,128,8,128]{3,1,2,0:T(8,128)(2,1)S(1)}, bf16[2,128,8,128]{3,1,2,0:T(8,128)(2,1)S(1)}, u32[]{:S(2)}, u32[]{:S(2)}) collective-permute-start(bf16[2,128,8,128]{3,1,2,0:T(8,128)(2,1)S(1)} %pad_maximum_fusion.29), channel_id=1, source_target_pairs={{24,0},{26,2},{28,4},{30,6},{25,1},{27,3},{29,5},{31,7}} | collective-permute-start | bytes 1572872 | tf_op jit(solution)/shard_map/ppermute | solution.py:18
  427.1 77.3 %collective-permute-start.26 = (bf16[2,128,8,128]{3,1,2,0:T(8,128)(2,1)}, bf16[2,128,8,128]{3,1,2,0:T(8,128)(2,1)}, u32[]{:S(2)}, u32[]{:S(2)}) collective-permute-start(bf16[2,128,8,128]{3,1,2,0:T(8,128)(2,1)} %pad_maximum_fusion.28), channel_id=1, source_target_pairs={{22,0},{24,2},{26,4},{28,6},{30,8},{23,1},{25,3},{27,5},{29,7},{31... | collective-permute-start | bytes 1572872 | tf_op jit(solution)/shard_map/ppermute | solution.py:18
  430.6 78.0 %collective-permute-start.25 = (bf16[2,128,8,128]{3,1,2,0:T(8,128)(2,1)}, bf16[2,128,8,128]{3,1,2,0:T(8,128)(2,1)}, u32[]{:S(2)}, u32[]{:S(2)}) collective-permute-start(bf16[2,128,8,128]{3,1,2,0:T(8,128)(2,1)} %pad_maximum_fusion.27), channel_id=1, source_target_pairs={{20,0},{22,2},{24,4},{26,6},{28,8},{30,10},{21,1},{23,3},{25,5},{2... | collective-permute-start | bytes 1572872 | tf_op jit(solution)/shard_map/ppermute | solution.py:18
  431.9 89.0 %collective-permute-start.24 = (bf16[2,128,8,128]{3,1,2,0:T(8,128)(2,1)}, bf16[2,128,8,128]{3,1,2,0:T(8,128)(2,1)}, u32[]{:S(2)}, u32[]{:S(2)}) collective-permute-start(bf16[2,128,8,128]{3,1,2,0:T(8,128)(2,1)} %pad_maximum_fusion.26), channel_id=1, source_target_pairs={{18,0},{20,2},{22,4},{24,6},{26,8},{28,10},{30,12},{19,1},{21,3},{... | collective-permute-start | bytes 1572872 | tf_op jit(solution)/shard_map/ppermute | solution.py:18
  433.2 145.2 %collective-permute-start.23 = (bf16[2,128,8,128]{3,1,2,0:T(8,128)(2,1)}, bf16[2,128,8,128]{3,1,2,0:T(8,128)(2,1)}, u32[]{:S(2)}, u32[]{:S(2)}) collective-permute-start(bf16[2,128,8,128]{3,1,2,0:T(8,128)(2,1)} %pad_maximum_fusion.25), channel_id=1, source_target_pairs={{16,0},{18,2},{20,4},{22,6},{24,8},{26,10},{28,12},{30,14},{17,1},... | collective-permute-start | bytes 1572872 | tf_op jit(solution)/shard_map/ppermute | solution.py:18
  491.2 96.4 %collective-permute-start.22 = (bf16[2,128,8,128]{3,1,2,0:T(8,128)(2,1)}, bf16[2,128,8,128]{3,1,2,0:T(8,128)(2,1)}, u32[]{:S(2)}, u32[]{:S(2)}) collective-permute-start(bf16[2,128,8,128]{3,1,2,0:T(8,128)(2,1)} %pad_maximum_fusion.24), channel_id=1, source_target_pairs={{14,0},{16,2},{18,4},{20,6},{22,8},{24,10},{26,12},{28,14},{30,16}... | collective-permute-start | bytes 1572872 | tf_op jit(solution)/shard_map/ppermute | solution.py:18
  504.4 87.9 %collective-permute-start.21 = (bf16[2,128,8,128]{3,1,2,0:T(8,128)(2,1)S(1)}, bf16[2,128,8,128]{3,1,2,0:T(8,128)(2,1)S(1)}, u32[]{:S(2)}, u32[]{:S(2)}) collective-permute-start(bf16[2,128,8,128]{3,1,2,0:T(8,128)(2,1)S(1)} %pad_maximum_fusion.23), channel_id=1, source_target_pairs={{12,0},{14,2},{16,4},{18,6},{20,8},{22,10},{24,12},{26,14},{28,16}... | collective-permute-start | bytes 1572872 | tf_op jit(solution)/shard_map/ppermute | solution.py:18
  508.6 88.6 %collective-permute-start.19 = (bf16[2,256,8,128]{3,1,2,0:T(8,128)(2,1)S(1)}, bf16[2,256,8,128]{3,1,2,0:T(8,128)(2,1)S(1)}, u32[]{:S(2)}, u32[]{:S(2)}) collective-permute-start(bf16[2,256,8,128]{3,1,2,0:T(8,128)(2,1)S(1)} %copy-done.53), channel_id=1, source_target_pairs={{8,0},{10,2},{12,4},{14,6},{16,8},{18,10},{20,12},{22,14},{24,16},... | collective-permute-start | bytes 3145736 | tf_op jit(solution)/shard_map/ppermute | solution.py:18
  521.0 88.6 %collective-permute-start.18 = (bf16[2,256,8,128]{3,1,2,0:T(8,128)(2,1)S(1)}, bf16[2,256,8,128]{3,1,2,0:T(8,128)(2,1)S(1)}, u32[]{:S(2)}, u32[]{:S(2)}) collective-permute-start(bf16[2,256,8,128]{3,1,2,0:T(8,128)(2,1)S(1)} %copy-done.52), channel_id=1, source_target_pairs={{6,0},{8,2},{10,4},{12,6},{14,8},{16,10},{18,12},{20,14},{22,16},{... | collective-permute-start | bytes 3145736 | tf_op jit(solution)/shard_map/ppermute | solution.py:18
  578.4 70.2 %collective-permute-start.17 = (bf16[2,256,8,128]{3,1,2,0:T(8,128)(2,1)S(1)}, bf16[2,256,8,128]{3,1,2,0:T(8,128)(2,1)S(1)}, u32[]{:S(2)}, u32[]{:S(2)}) collective-permute-start(bf16[2,256,8,128]{3,1,2,0:T(8,128)(2,1)S(1)} %copy-done.51), channel_id=1, source_target_pairs={{4,0},{6,2},{8,4},{10,6},{12,8},{14,10},{16,12},{18,14},{20,16},{2... | collective-permute-start | bytes 3145736 | tf_op jit(solution)/shard_map/ppermute | solution.py:18
  587.5 72.1 %collective-permute-start.16 = (bf16[2,256,8,128]{3,1,2,0:T(8,128)(2,1)S(1)}, bf16[2,256,8,128]{3,1,2,0:T(8,128)(2,1)S(1)}, u32[]{:S(2)}, u32[]{:S(2)}) collective-permute-start(bf16[2,256,8,128]{3,1,2,0:T(8,128)(2,1)S(1)} %copy-done.50), channel_id=1, source_target_pairs={{2,0},{4,2},{6,4},{8,6},{10,8},{12,10},{14,12},{16,14},{18,16},{20... | collective-permute-start | bytes 3145736 | tf_op jit(solution)/shard_map/ppermute | solution.py:18
  (198 other events, 5649.8 us)
Sparse Core Ops, SparseCore 0:
  26.3 54.6 all-gather.1
where the time goes:
time: 686 us; the launch traced here: 677 us
  waiting for transfers between devices  251 us (37%)
  matrix products  195 us (28%)
  starting transfers between devices  95.4 us (14%)
  other arithmetic  60.6 us (9%)
  local copies, waits for them, and re-layouts  55.1 us (8%)
  between operations  19.7 us (3%)
    ppermute x32, waiting for transfers between devices, passed_along(): return lax.ppermute(value, axis, pairs)  251 us
    dot_general x132, matrix products, product(): jnp.einsum(pattern, left_operand, right_operand, preferred_element_type=j...  190 us
    ppermute x32, starting transfers between devices, passed_along(): return lax.ppermute(value, axis, pairs)  95.4 us
    reduce_sum x8, other arithmetic, shard_grads(): total_here = total_here + jnp.sum(weights, axis=-1)  29.9 us
    unnamed x440, local copies, waits for them, and re-layouts  19.2 us
    another operation x16, local copies, waits for them, and re-layouts, put_half(): stacked = jnp.stack([first_half, second_half], axis=-3)  15.4 us
    slice x6, local copies, waits for them, and re-layouts, take_half(): paired[..., 0, :, :]  13.7 us
  transfers between devices with their start and end apart: 33, of which 14 were waited for; matrix products, arithmetic and copies ran while one was open for 18% of the time, Pallas kernels for 0%

commit v1 on v0

v1 whole, which is shorter than its diff:
```python
import math

import jax
import jax.numpy as jnp
from jax import lax
from jax.sharding import PartitionSpec as P

REACH_SHORT = 4
REACH_LONG = 16


VERY_NEGATIVE = -1e30


def passed_along(value, axis, by):
    devices = lax.axis_size(axis)
    pairs = [(i, i + by) for i in range(devices) if 0 <= i + by < devices]
    return lax.ppermute(value, axis, pairs)


def take_half(tensor, parity):
    layout = tensor.shape
    paired = tensor.reshape(layout[:-3] + (layout[-3] // 2, 2) + layout[-2:])
    return jnp.where((parity == 0)[:, None], paired[..., 0, :, :], paired[..., 1, :, :])


def put_half(tensor, parity):
    zero_fill = jnp.zeros_like(tensor)
    first_half = jnp.where((parity == 0)[:, None], tensor, zero_fill)
    second_half = jnp.where((parity == 1)[:, None], tensor, zero_fill)
    stacked = jnp.stack([first_half, second_half], axis=-3)
    return stacked.reshape(tensor.shape[:-3] + (2 * tensor.shape[-3],) + tensor.shape[-2:])


def stat_half(tensor, parity):
    paired = tensor.reshape(tensor.shape[:-1] + (tensor.shape[-1] // 2, 2))
    return jnp.where((parity == 0)[:, None], paired[..., 0], paired[..., 1])


def stat_put(tensor, parity, fill_value):
    filler = jnp.full_like(tensor, fill_value)
    first_half = jnp.where((parity == 0)[:, None], tensor, filler)
    second_half = jnp.where((parity == 1)[:, None], tensor, filler)
    return jnp.stack([first_half, second_half], axis=-1).reshape(
        tensor.shape[:-1] + (2 * tensor.shape[-1],)
    )


def segment_of(positions, lengths):
    seg_ends = jnp.cumsum(lengths)
    return jnp.sum((positions[..., None] >= seg_ends).astype(jnp.int32), axis=-1)


def row_positions(shard_index, tok_dev, stride, offset, row_count):
    return (
        shard_index * tok_dev
        + stride * jnp.arange(row_count, dtype=jnp.int32)[None, :]
        + offset[:, None]
    )


def window_positions(shard_index, distances, tok_dev, stride, offset, row_count):
    return jnp.concatenate(
        [row_positions(shard_index + d, tok_dev, stride, offset, row_count) for d in distances],
        axis=1,
    )


def pair_mask(query_pos, key_pos, lengths, total):
    query_seg = segment_of(query_pos, lengths)
    key_seg = segment_of(key_pos, lengths)
    causal = key_pos[:, None, :] <= query_pos[:, :, None]
    same_seg = key_seg[:, None, :] == query_seg[:, :, None]
    valid = (key_pos[:, None, :] >= 0) & (query_pos[:, :, None] < total)
    return causal & same_seg & valid


def product(pattern, left_operand, right_operand):
    return jnp.einsum(pattern, left_operand, right_operand, preferred_element_type=jnp.float32)


def query_side(shard_index, total, q_rows, g_rows, near_kv, far_kv, head_phase, seg_short, seg_long):
    rows_short, head_count, head_width = q_rows.shape
    tok_dev = 2 * rows_short
    scale = 1.0 / math.sqrt(head_width)
    par_short = head_phase % 2
    par_long = head_phase // 2
    levels = [
        (q_rows, g_rows, near_kv, 2, par_short, seg_short),
        (take_half(q_rows, par_long), take_half(g_rows, par_long), far_kv, 4, head_phase, seg_long),
    ]
    stored = []
    peaks = []
    for query_here, grad_here, window, stride, offset, lengths in levels:
        row_count = query_here.shape[0]
        keys = jnp.concatenate([w[0] for w in window], axis=0)
        values = jnp.concatenate([w[1] for w in window], axis=0)
        query_pos = row_positions(shard_index, tok_dev, stride, offset, row_count)
        key_pos = window_positions(
            shard_index, [-d for d in range(len(window))], tok_dev, stride, offset, row_count
        )
        live = pair_mask(query_pos, key_pos, lengths, total)
        scores = jnp.where(live, product("qhd,khd->hqk", query_here, keys) * scale, VERY_NEGATIVE)
        peaks.append(jnp.max(scores, axis=-1))
        stored.append((live, scores, keys, values))
    top_short = jnp.maximum(peaks[0], stat_put(peaks[1], par_long, VERY_NEGATIVE))
    level_tops = [top_short, stat_half(top_short, par_long)]
    totals = []
    numerators = []
    for level_index, (live, scores, keys, values) in enumerate(stored):
        weights = jnp.where(live, jnp.exp(scores - level_tops[level_index][:, :, None]), 0.0)
        totals.append(jnp.sum(weights, axis=-1))
        numerators.append(product("hqk,khd->qhd", weights.astype(jnp.bfloat16), values))
    denominator = totals[0] + stat_put(totals[1], par_long, 0.0)
    attended = (numerators[0] + put_half(numerators[1], par_long)) / jnp.transpose(denominator)[
        :, :, None
    ]
    delta_rows = jnp.transpose(jnp.sum(g_rows.astype(jnp.float32) * attended, axis=-1))
    inverse = 1.0 / denominator
    level_inverse = [inverse, stat_half(inverse, par_long)]
    level_delta = [delta_rows, stat_half(delta_rows, par_long)]
    grads = []
    for level_index, (live, scores, keys, values) in enumerate(stored):
        grad_here = levels[level_index][1]
        probability = (
            jnp.where(live, jnp.exp(scores - level_tops[level_index][:, :, None]), 0.0)
            * level_inverse[level_index][:, :, None]
        )
        grad_probs = product("qhd,khd->hqk", grad_here, values)
        grad_scores = (probability * (grad_probs - level_delta[level_index][:, :, None])).astype(
            jnp.bfloat16
        )
        grads.append(product("hqk,khd->qhd", grad_scores, keys) * scale)
    grad_query = grads[0] + put_half(grads[1], par_long)
    return grad_query, jnp.stack([top_short, inverse, delta_rows])


def key_side(shard_index, total, k_rows, v_rows, near_qg, near_stats, far_qg, far_stats, head_phase, seg_short, seg_long):
    rows_short, head_count, head_width = k_rows.shape
    tok_dev = 2 * rows_short
    scale = 1.0 / math.sqrt(head_width)
    par_short = head_phase % 2
    par_long = head_phase // 2
    levels = [
        (k_rows, v_rows, near_qg, near_stats, 2, par_short, seg_short),
        (take_half(k_rows, par_long), take_half(v_rows, par_long), far_qg, far_stats, 4, head_phase, seg_long),
    ]
    results = []
    for key_here, value_here, window, stats, stride, offset, lengths in levels:
        row_count = key_here.shape[0]
        queries = jnp.concatenate([w[0] for w in window], axis=0)
        grads = jnp.concatenate([w[1] for w in window], axis=0)
        row_stats = jnp.concatenate(stats, axis=-1)
        key_pos = row_positions(shard_index, tok_dev, stride, offset, row_count)
        query_pos = window_positions(
            shard_index, list(range(len(window))), tok_dev, stride, offset, row_count
        )
        live = pair_mask(query_pos, key_pos, lengths, total)
        scores = jnp.where(live, product("qhd,khd->hqk", queries, key_here) * scale, VERY_NEGATIVE)
        probability = (
            jnp.where(live, jnp.exp(scores - row_stats[0][:, :, None]), 0.0)
            * row_stats[1][:, :, None]
        )
        grad_probs = product("qhd,khd->hqk", grads, value_here)
        grad_scores = (probability * (grad_probs - row_stats[2][:, :, None])).astype(jnp.bfloat16)
        grad_key = product("hqk,qhd->khd", grad_scores, queries) * scale
        grad_value = product("hqk,qhd->khd", probability.astype(jnp.bfloat16), grads)
        results.append((grad_key, grad_value))
    grad_key = results[0][0] + put_half(results[1][0], par_long)
    grad_value = results[0][1] + put_half(results[1][1], par_long)
    return grad_key, grad_value


def shards(
    queries,
    key_vectors,
    value_vectors,
    grad_mixed,
    out_weight,
    head_phase,
    segments_short,
    segments_long,
):
    shard_index = lax.axis_index("seq")
    devices = lax.axis_size("seq")
    tok_dev = queries.shape[1]
    total = devices * tok_dev
    head_count = head_phase.shape[0]
    head_width = queries.shape[2] // head_count
    par_short = head_phase % 2
    par_long = head_phase // 2

    def split_rows(tensor):
        return take_half(tensor.reshape(tok_dev, head_count, head_width), par_short)

    near_steps = [d for d in range(1, REACH_SHORT + 1) if d < devices]
    far_steps = [d for d in range(REACH_SHORT + 1, REACH_LONG + 1) if d < devices]

    own_kv = jnp.stack([split_rows(key_vectors[0]), split_rows(value_vectors[0])])
    own_kv_long = take_half(own_kv, par_long)
    near_kv = [own_kv] + [passed_along(own_kv, "seq", d) for d in near_steps]
    far_kv = [take_half(w, par_long) for w in near_kv] + [
        passed_along(own_kv_long, "seq", d) for d in far_steps
    ]

    q_rows = split_rows(queries[0])
    grad_out = jnp.einsum(
        "td,rd->tr",
        grad_mixed[0],
        lax.all_gather(out_weight, "fsdp", axis=0, tiled=True),
        preferred_element_type=jnp.float32,
    ).astype(jnp.bfloat16)
    g_rows = split_rows(grad_out)
    own_qg = jnp.stack([q_rows, g_rows])
    own_qg_long = take_half(own_qg, par_long)
    near_qg = [own_qg] + [passed_along(own_qg, "seq", -d) for d in near_steps]
    far_qg = [take_half(w, par_long) for w in near_qg] + [
        passed_along(own_qg_long, "seq", -d) for d in far_steps
    ]

    grad_query, own_stats = query_side(
        shard_index, total, q_rows, g_rows, near_kv, far_kv, head_phase, segments_short, segments_long
    )
    own_stats_long = stat_half(own_stats, par_long)
    near_stats = [own_stats] + [passed_along(own_stats, "seq", -d) for d in near_steps]
    far_stats = [stat_half(s, par_long) for s in near_stats] + [
        passed_along(own_stats_long, "seq", -d) for d in far_steps
    ]
    grad_key, grad_value = key_side(
        shard_index,
        total,
        own_kv[0],
        own_kv[1],
        near_qg,
        near_stats,
        far_qg,
        far_stats,
        head_phase,
        segments_short,
        segments_long,
    )

    def to_tokens(rows_here):
        return put_half(rows_here, par_short).reshape(1, tok_dev, head_count * head_width)

    return (
        to_tokens(grad_query.astype(jnp.bfloat16)),
        to_tokens(grad_key.astype(jnp.bfloat16)),
        to_tokens(grad_value.astype(jnp.bfloat16)),
    )


def solution(mesh):
    placed = (
        P("fsdp", "seq", None),
        P("fsdp", "seq", None),
        P("fsdp", "seq", None),
        P("fsdp", "seq", None),
        P("fsdp", None),
        P(),
        P(),
        P(),
    )
    return jax.shard_map(
        shards,
        mesh=mesh,
        in_specs=placed,
        out_specs=(P("fsdp", "seq", None), P("fsdp", "seq", None), P("fsdp", "seq", None)),
        check_vma=False,
    )
```

time: 686 us -> 696 us (1.015)
  the two profiles are of different devices: /device:TPU:5 before, /device:TPU:0 now
where the time goes in v1:
time: 696 us; the launch traced here: 686 us
  waiting for transfers between devices  245 us (35%)
  starting transfers between devices  150 us (22%)
  matrix products  132 us (19%)
  local copies, waits for them, and re-layouts  98.5 us (14%)
  other arithmetic  43.2 us (6%)
  between operations  17.6 us (3%)
    ppermute x45, waiting for transfers between devices, passed_along(): return lax.ppermute(value, axis, pairs)  212 us
    ppermute x45, starting transfers between devices, passed_along(): return lax.ppermute(value, axis, pairs)  150 us
    dot_general x14, matrix products, product(): jnp.einsum(pattern, left_operand, right_operand, preferred_element_type=j...  127 us
    unnamed x300, local copies, waits for them, and re-layouts  59 us
    all_gather x1, waiting for transfers between devices, shards(): lax.all_gather(out_weight, 'fsdp', axis=0, tiled=True)  32.8 us
    slice x10, local copies, waits for them, and re-layouts, take_half(): paired[..., 0, :, :]  18.5 us
  transfers between devices with their start and end apart: 46, of which 13 were waited for; matrix products, arithmetic and copies ran while one was open for 26% of the time, Pallas kernels for 0%

profile of v1, /device:TPU:0, one launch (start us, length us, event | category | flops | bytes accessed | tf_op | source)
XLA Modules:
  0.0 685.7 jit_solution(12506734566702895928)
XLA Ops:
  9.3 2.5 copy.429
  16.9 2.8 fusion.190
  21.7 2.5 copy.428
  36.3 32.8 %all-gather.2.cloned.1.call-done = bf16[1024,2048]{1,0:T(8,128)(2,1)} async-done(((bf16[512,2048]{1,0:T(8,128)(2,1)}), bf16[1024,2048]{1,0:T(8,128)(2,1)}) %all-gather.2.cloned.1.call-update) | async-done | bytes 4194320 | tf_op jit(solution)/shard_map/all_gather | solution.py:210
  69.1 4.6 fusion.19
  77.8 3.7 collective-permute-start.1
  81.5 4.3 collective-permute-start.2
  85.8 3.3 collective-permute-start.3
  95.3 17.4 %collective-permute-done.3 = bf16[2,256,8,128]{3,1,2,0:T(8,128)(2,1)S(1)} collective-permute-done((bf16[2,256,8,128]{3,1,2,0:T(8,128)(2,1)S(1)}, bf16[2,256,8,128]{3,1,2,0:T(8,128)(2,1)S(1)}, u32[]{:S(2)}, u32[]{:S(2)}) %collective-permute-start.3) | collective-permute-done | bytes 1048608 | tf_op jit(solution)/shard_map/ppermute | solution.py:18
  115.9 9.1 %collective-permute-done.2 = bf16[2,256,8,128]{3,1,2,0:T(8,128)(2,1)S(1)} collective-permute-done((bf16[2,256,8,128]{3,1,2,0:T(8,128)(2,1)S(1)}, bf16[2,256,8,128]{3,1,2,0:T(8,128)(2,1)S(1)}, u32[]{:S(2)}, u32[]{:S(2)}) %collective-permute-start.2) | collective-permute-done | bytes 1048608 | tf_op jit(solution)/shard_map/ppermute | solution.py:18
  131.6 53.8 %collective-permute-done.17 = bf16[2,256,8,128]{3,1,2,0:T(8,128)(2,1)S(1)} collective-permute-done((bf16[2,256,8,128]{3,1,2,0:T(8,128)(2,1)S(1)}, bf16[2,256,8,128]{3,1,2,0:T(8,128)(2,1)S(1)}, u32[]{:S(2)}, u32[]{:S(2)}) %collective-permute-start.17) | collective-permute-done | bytes 1048608 | tf_op jit(solution)/shard_map/ppermute | solution.py:18
  188.4 2.1 collective-permute-start.4
  190.5 2.1 collective-permute-start.5
  194.5 2.0 constant_dynamic-update-slice_fusion.54
  196.5 2.1 collective-permute-start.6
  200.5 2.1 collective-permute-start.7
  204.6 31.4 %collective-permute-start.8 = (bf16[2,128,8,128]{3,1,2,0:T(8,128)(2,1)}, bf16[2,128,8,128]{3,1,2,0:T(8,128)(2,1)}, u32[]{:S(2)}, u32[]{:S(2)}) collective-permute-start(bf16[2,128,8,128]{3,1,2,0:T(8,128)(2,1)} %get-tuple-element.207), channel_id=1, source_target_pairs={{0,18},{2,20},{4,22},{6,24},{8,26},{10,28},{12,30},{1,19},{3,21},{... | collective-permute-start | bytes 1572872 | tf_op jit(solution)/shard_map/ppermute | solution.py:18
  244.1 5.6 fusion.170
  254.9 6.7 fusion
  265.8 2.0 constant_dynamic-update-slice_fusion.49
  269.1 2.0 constant_dynamic-update-slice_fusion.48
  272.9 2.0 constant_dynamic-update-slice_fusion.47
  274.9 33.8 %collective-permute-start.12 = (bf16[2,128,8,128]{3,1,2,0:T(8,128)(2,1)}, bf16[2,128,8,128]{3,1,2,0:T(8,128)(2,1)S(1)}, u32[]{:S(2)}, u32[]{:S(2)}) collective-permute-start(bf16[2,128,8,128]{3,1,2,0:T(8,128)(2,1)} %get-tuple-element.207), channel_id=1, source_target_pairs={{0,26},{2,28},{4,30},{1,27},{3,29},{5,31}} | collective-permute-start | bytes 1572872 | tf_op jit(solution)/shard_map/ppermute | solution.py:18
  308.7 2.0 constant_dynamic-update-slice_fusion.46
  310.7 15.0 %collective-permute-start.13 = (bf16[2,128,8,128]{3,1,2,0:T(8,128)(2,1)}, bf16[2,128,8,128]{3,1,2,0:T(8,128)(2,1)S(1)}, u32[]{:S(2)}, u32[]{:S(2)}) collective-permute-start(bf16[2,128,8,128]{3,1,2,0:T(8,128)(2,1)} %get-tuple-element.207), channel_id=1, source_target_pairs={{0,28},{2,30},{1,29},{3,31}} | collective-permute-start | bytes 1572872 | tf_op jit(solution)/shard_map/ppermute | solution.py:18
  327.7 4.5 collective-permute-start.14
  341.7 3.9 collective-permute-done.14
  347.9 5.5 fusion.1
  353.6 5.8 fusion.41
  359.7 7.7 %fusion.12 = f32[8,256]{1,0:T(8,128)S(1)} fusion(f32[8,256]{1,0:T(8,128)S(1)} %max.28, f32[8,256,1280]{2,1,0:T(8,128)} %get-tuple-element.227, pred[8,256]{1,0:T(8,128)(4,1)S(1)} %copy-done.95, pred[8,1280]{1,0:T(8,128)(4,1)S(1)} %broadcast_compare_fusion.3, s32[8,256]{1,0:T(8,128)S(1)} %copy-done.75, s32[8,1280]{1,0:T(8,128)S(1)} %get-tuple-element.4, ...), kind=kLoop, calls=%fused_computation.24 | loop fusion | flops 26212352 | bytes 10612736 | tf_op jit(solution)/shard_map/reduce_sum | solution.py:112
  369.2 7.2 %select_bitcast_fusion.13 = (f32[128,1,8,128]{3,0,2,1:T(8,128)S(1)}, f32[128,1,8,128]{3,0,2,1:T(8,128)S(1)}) fusion(pred[8]{0:T(512)(128)(4,1)S(1)} %get-tuple-element.230, pred[8]{0:T(512)(128)(4,1)S(1)} %copy-done.98, bf16[2048,8,128]{2,0,1:T(8,128)(2,1)} %get-tuple-element.97, f32[8,128]{1,0:T(8,128)S(1)} %fusion.103, f32[8,128,2048]{2,1,0:T(8,128)} %copy-done.4, ...), kind=kOutput, calls=%fused_computation.156 | convolution fusion | flops 558104576 | bytes 13792272 | tf_op jit(solution)/shard_map/hqk,khd->qhd/dot_general | solution.py:79
  378.5 6.8 multiply_reduce_fusion
  391.0 2.0 constant_dynamic-update-slice_fusion.124
  395.3 55.4 %collective-permute-done.26 = bf16[2,128,8,128]{3,1,2,0:T(8,128)(2,1)} collective-permute-done((bf16[2,128,8,128]{3,1,2,0:T(8,128)(2,1)S(1)}, bf16[2,128,8,128]{3,1,2,0:T(8,128)(2,1)}, u32[]{:S(2)}, u32[]{:S(2)}) %collective-permute-start.26) | collective-permute-done | bytes 524320 | tf_op jit(solution)/shard_map/ppermute | solution.py:18
  453.9 15.4 %collective-permute-done.27 = bf16[2,128,8,128]{3,1,2,0:T(8,128)(2,1)} collective-permute-done((bf16[2,128,8,128]{3,1,2,0:T(8,128)(2,1)S(1)}, bf16[2,128,8,128]{3,1,2,0:T(8,128)(2,1)}, u32[]{:S(2)}, u32[]{:S(2)}) %collective-permute-start.27) | collective-permute-done | bytes 524320 | tf_op jit(solution)/shard_map/ppermute | solution.py:18
  470.6 2.0 constant_dynamic-update-slice_fusion.121
  476.6 18.2 %collective-permute-done.29 = bf16[2,128,8,128]{3,1,2,0:T(8,128)(2,1)} collective-permute-done((bf16[2,128,8,128]{3,1,2,0:T(8,128)(2,1)S(1)}, bf16[2,128,8,128]{3,1,2,0:T(8,128)(2,1)}, u32[]{:S(2)}, u32[]{:S(2)}) %collective-permute-start.29) | collective-permute-done | bytes 524320 | tf_op jit(solution)/shard_map/ppermute | solution.py:18
  506.8 6.7 fusion.87
  530.5 13.3 %multiply_convert_fusion.clone.12 = bf16[8,1280,256]{2,1,0:T(8,128)(2,1)} fusion(bf16[1280,8,128]{2,0,1:T(8,128)(2,1)} %get-tuple-element.11, f32[8,1280]{1,0:T(8,128)S(1)} %get-tuple-element.145, f32[8,1280]{1,0:T(8,128)S(1)} %get-tuple-element.146, f32[8,1280]{1,0:T(8,128)S(1)} %get-tuple-element.144, ...), kind=kOutput, calls=%fused_computation.clone.clone.clone.clone.clone.clone.clone.clone.clone.clone.cl... | convolution fusion | flops 705429504 | bytes 19632136 | tf_op jit(solution)/shard_map/qhd,khd->hqk/dot_general | solution.py:79
  548.0 26.5 %collective-permute-done.37 = f32[3,8,128]{1,2,0:T(8,128)S(1)} collective-permute-done((f32[3,8,128]{1,2,0:T(8,128)S(1)}, f32[3,8,128]{1,2,0:T(8,128)S(1)}, u32[]{:S(2)}, u32[]{:S(2)}) %collective-permute-start.37) | collective-permute-done | bytes 12320 | tf_op jit(solution)/shard_map/ppermute | solution.py:18
  579.5 3.8 collective-permute-done.42
  583.3 6.9 %collective-permute-done.43 = f32[3,8,128]{1,2,0:T(8,128)S(1)} collective-permute-done((f32[3,8,128]{1,2,0:T(8,128)S(1)}, f32[3,8,128]{1,2,0:T(8,128)S(1)}, u32[]{:S(2)}, u32[]{:S(2)}) %collective-permute-start.43) | collective-permute-done | bytes 12320 | tf_op jit(solution)/shard_map/ppermute | solution.py:18
  591.0 17.5 %fusion.6 = f32[8,128,128]{1,2,0:T(8,128)} fusion(bf16[2048,8,128]{2,0,1:T(8,128)(2,1)} %get-tuple-element.59, f32[8,2048,128]{2,1,0:T(8,128)} %fusion.87, f32[8,2048]{1,0:T(8,128)S(1)} %get-tuple-element.141, f32[8,2048]{1,0:T(8,128)S(1)} %get-tuple-element.139, s32[8,2048]{1,0:T(8,128)S(1)} %copy-done.57, s32[8,128]{1,0:T(8,128)S(1)} %copy-done.88, ...), kind=kOutput, calls=%fused_computation.18 | convolution fusion | flops 559939584 | bytes 13394944 | tf_op jit(solution)/shard_map/hqk,qhd->khd/dot_general | solution.py:79
  608.5 15.9 %multiply_convert_fusion.2.clone.6 = bf16[8,2048,128]{2,1,0:T(8,128)(2,1)S(1)} fusion(bf16[2048,8,128]{2,0,1:T(8,128)(2,1)S(1)} %copy-done.91, f32[8,2048]{1,0:T(8,128)S(1)} %get-tuple-element.140, f32[8,2048]{1,0:T(8,128)S(1)} %get-tuple-element.141, f32[8,2048]{1,0:T(8,128)S(1)} %get-tuple-element.139, ...), kind=kOutput, calls=%fused_computation.7.clone.clone.clone.clone.clone.1 | convolution fusion | flops 564264960 | bytes 17654792 | tf_op jit(solution)/shard_map/qhd,khd->hqk/dot_general | solution.py:79
  624.6 3.6 fusion.47
  628.3 10.8 %select_bitcast_fusion.11 = (f32[128,1,8,128]{3,0,2,1:T(8,128)S(1)}, f32[128,1,8,128]{3,0,2,1:T(8,128)S(1)}, f32[128,1,8,128]{3,0,2,1:T(8,128)}, f32[128,1,8,128...) fusion(pred[8]{0:T(512)(128)(4,1)S(1)} %copy-done.61, pred[8]{0:T(512)(128)(4,1)S(1)} %copy-done.99, ...), kind=kOutput, calls=%fused_computation.154 | convolution fusion | flops 1102053376 | bytes 21666304 | tf_op jit(solution)/shard_map/hqk,khd->qhd/dot_general | solution.py:79
  642.3 13.7 %fusion.44 = bf16[256,8,128]{2,0,1:T(8,128)(2,1)} fusion(f32[256,8,128]{2,0,1:T(8,128)S(1)} %bitcast.817, bf16[1280,8,128]{2,0,1:T(8,128)(2,1)S(1)} %copy-done.43, f32[8,1280]{1,0:T(8,128)S(1)} %copy-done.68, f32[8,1280]{1,0:T(8,128)S(1)} %copy-done.66, f32[8,1280,256]{2,1,0:T(8,128)} %fusion.170, pred[8,1280]{1,0:T(8,128)(4,1)S(1)} %copy-done.92, ...), kind=kOutput, calls=%fused_computation.44 | convolution fusion | flops 700448768 | bytes 14872576 | tf_op jit(solution)/shard_map/hqk,qhd->khd/dot_general | solution.py:79
  657.9 12.0 %select_bitcast_fusion.9 = (bf16[256,1,8,128]{3,0,2,1:T(8,128)(2,1)}, bf16[256,1,8,128]{3,0,2,1:T(8,128)(2,1)}, bf16[256,1,8,128]{3,0,2,1:T(8,128)(2,1)S(1)}, bf...) fusion(pred[8]{0:T(512)(128)(4,1)S(1)} %copy-done.79, ...), kind=kOutput, calls=%fused_computation.152 | convolution fusion | flops 1378615296 | bytes 21630992 | tf_op jit(solution)/shard_map/hqk,khd->qhd/dot_general | solution.py:79
  (542 shorter events, 155.4 us)
Async XLA Ops:
  7.2 61.9 %all-gather.2.cloned.1.call-start = ((), (), s32[]{:S(2)}) async-start(), calls=%async_computation | async-start | bytes 6291456 | tf_op jit(solution)/shard_map/all_gather | solution.py:210
  13.1 356.1 %copy-start.58 = (pred[8]{0:T(512)(128)(4,1)}, pred[8]{0:T(512)(128)(4,1)S(1)}, u32[]{:S(2)}) copy-start(pred[8]{0:T(512)(128)(4,1)S(1)} %get-tuple-element.230) | copy-start | bytes 28
  13.1 364.2 %copy-start.52 = (s32[8,256]{1,0:T(8,128)}, s32[8,256]{1,0:T(8,128)S(1)}, u32[]{:S(2)}) copy-start(s32[8,256]{1,0:T(8,128)S(1)} %get-tuple-element.165) | copy-start | bytes 24580
  76.2 114.4 %collective-permute-start = (bf16[2,256,8,128]{3,1,2,0:T(8,128)(2,1)S(1)}, bf16[2,256,8,128]{3,1,2,0:T(8,128)(2,1)S(1)}, u32[]{:S(2)}, u32[]{:S(2)}) collective-permute-start(bf16[2,256,8,128]{3,1,2,0:T(8,128)(2,1)S(1)} %pad_maximum_fusion), channel_id=1, source_target_pairs={{0,2},{2,4},{4,6},{6,8},{8,10},{10,12},{12,14},{14,16},{16,18},{18... | collective-permute-start | bytes 3145736 | tf_op jit(solution)/shard_map/ppermute | solution.py:18
  77.8 50.3 %collective-permute-start.1 = (bf16[2,256,8,128]{3,1,2,0:T(8,128)(2,1)S(1)}, bf16[2,256,8,128]{3,1,2,0:T(8,128)(2,1)S(1)}, u32[]{:S(2)}, u32[]{:S(2)}) collective-permute-start(bf16[2,256,8,128]{3,1,2,0:T(8,128)(2,1)S(1)} %pad_maximum_fusion), channel_id=1, source_target_pairs={{0,4},{2,6},{4,8},{6,10},{8,12},{10,14},{12,16},{14,18},{16,20},{1... | collective-permute-start | bytes 3145736 | tf_op jit(solution)/shard_map/ppermute | solution.py:18
  81.5 43.4 %collective-permute-start.2 = (bf16[2,256,8,128]{3,1,2,0:T(8,128)(2,1)S(1)}, bf16[2,256,8,128]{3,1,2,0:T(8,128)(2,1)S(1)}, u32[]{:S(2)}, u32[]{:S(2)}) collective-permute-start(bf16[2,256,8,128]{3,1,2,0:T(8,128)(2,1)S(1)} %pad_maximum_fusion), channel_id=1, source_target_pairs={{0,6},{2,8},{4,10},{6,12},{8,14},{10,16},{12,18},{14,20},{16,22},{... | collective-permute-start | bytes 3145736 | tf_op jit(solution)/shard_map/ppermute | solution.py:18
  85.8 26.8 %collective-permute-start.3 = (bf16[2,256,8,128]{3,1,2,0:T(8,128)(2,1)S(1)}, bf16[2,256,8,128]{3,1,2,0:T(8,128)(2,1)S(1)}, u32[]{:S(2)}, u32[]{:S(2)}) collective-permute-start(bf16[2,256,8,128]{3,1,2,0:T(8,128)(2,1)S(1)} %pad_maximum_fusion), channel_id=1, source_target_pairs={{0,8},{2,10},{4,12},{6,14},{8,16},{10,18},{12,20},{14,22},{16,24},... | collective-permute-start | bytes 3145736 | tf_op jit(solution)/shard_map/ppermute | solution.py:18
  89.6 106.9 %collective-permute-start.18 = (bf16[2,256,8,128]{3,1,2,0:T(8,128)(2,1)S(1)}, bf16[2,256,8,128]{3,1,2,0:T(8,128)(2,1)S(1)}, u32[]{:S(2)}, u32[]{:S(2)}) collective-permute-start(bf16[2,256,8,128]{3,1,2,0:T(8,128)(2,1)S(1)} %pad_maximum_fusion.4), channel_id=1, source_target_pairs={{8,0},{10,2},{12,4},{14,6},{16,8},{18,10},{20,12},{22,14},{24,16},... | collective-permute-start | bytes 3145736 | tf_op jit(solution)/shard_map/ppermute | solution.py:18
  112.6 72.8 %collective-permute-start.17 = (bf16[2,256,8,128]{3,1,2,0:T(8,128)(2,1)S(1)}, bf16[2,256,8,128]{3,1,2,0:T(8,128)(2,1)S(1)}, u32[]{:S(2)}, u32[]{:S(2)}) collective-permute-start(bf16[2,256,8,128]{3,1,2,0:T(8,128)(2,1)S(1)} %pad_maximum_fusion.4), channel_id=1, source_target_pairs={{6,0},{8,2},{10,4},{12,6},{14,8},{16,10},{18,12},{20,14},{22,16},{... | collective-permute-start | bytes 3145736 | tf_op jit(solution)/shard_map/ppermute | solution.py:18
  124.9 75.6 %collective-permute-start.16 = (bf16[2,256,8,128]{3,1,2,0:T(8,128)(2,1)S(1)}, bf16[2,256,8,128]{3,1,2,0:T(8,128)(2,1)S(1)}, u32[]{:S(2)}, u32[]{:S(2)}) collective-permute-start(bf16[2,256,8,128]{3,1,2,0:T(8,128)(2,1)S(1)} %pad_maximum_fusion.4), channel_id=1, source_target_pairs={{4,0},{6,2},{8,4},{10,6},{12,8},{14,10},{16,12},{18,14},{20,16},{2... | collective-permute-start | bytes 3145736 | tf_op jit(solution)/shard_map/ppermute | solution.py:18
  128.2 76.4 %collective-permute-start.15 = (bf16[2,256,8,128]{3,1,2,0:T(8,128)(2,1)S(1)}, bf16[2,256,8,128]{3,1,2,0:T(8,128)(2,1)S(1)}, u32[]{:S(2)}, u32[]{:S(2)}) collective-permute-start(bf16[2,256,8,128]{3,1,2,0:T(8,128)(2,1)S(1)} %pad_maximum_fusion.4), channel_id=1, source_target_pairs={{2,0},{4,2},{6,4},{8,6},{10,8},{12,10},{14,12},{16,14},{18,16},{20... | collective-permute-start | bytes 3145736 | tf_op jit(solution)/shard_map/ppermute | solution.py:18
  188.4 76.1 %collective-permute-start.4 = (bf16[2,128,8,128]{3,1,2,0:T(8,128)(2,1)}, bf16[2,128,8,128]{3,1,2,0:T(8,128)(2,1)}, u32[]{:S(2)}, u32[]{:S(2)}) collective-permute-start(bf16[2,128,8,128]{3,1,2,0:T(8,128)(2,1)} %get-tuple-element.207), channel_id=1, source_target_pairs={{0,10},{2,12},{4,14},{6,16},{8,18},{10,20},{12,22},{14,24},{16,26}... | collective-permute-start | bytes 1572872 | tf_op jit(solution)/shard_map/ppermute | solution.py:18
  190.5 77.3 %collective-permute-start.5 = (bf16[2,128,8,128]{3,1,2,0:T(8,128)(2,1)}, bf16[2,128,8,128]{3,1,2,0:T(8,128)(2,1)}, u32[]{:S(2)}, u32[]{:S(2)}) collective-permute-start(bf16[2,128,8,128]{3,1,2,0:T(8,128)(2,1)} %get-tuple-element.207), channel_id=1, source_target_pairs={{0,12},{2,14},{4,16},{6,18},{8,20},{10,22},{12,24},{14,26},{16,28}... | collective-permute-start | bytes 1572872 | tf_op jit(solution)/shard_map/ppermute | solution.py:18
  196.5 74.6 %collective-permute-start.6 = (bf16[2,128,8,128]{3,1,2,0:T(8,128)(2,1)}, bf16[2,128,8,128]{3,1,2,0:T(8,128)(2,1)}, u32[]{:S(2)}, u32[]{:S(2)}) collective-permute-start(bf16[2,128,8,128]{3,1,2,0:T(8,128)(2,1)} %get-tuple-element.207), channel_id=1, source_target_pairs={{0,14},{2,16},{4,18},{6,20},{8,22},{10,24},{12,26},{14,28},{16,30}... | collective-permute-start | bytes 1572872 | tf_op jit(solution)/shard_map/ppermute | solution.py:18
  200.5 74.3 %collective-permute-start.7 = (bf16[2,128,8,128]{3,1,2,0:T(8,128)(2,1)}, bf16[2,128,8,128]{3,1,2,0:T(8,128)(2,1)}, u32[]{:S(2)}, u32[]{:S(2)}) collective-permute-start(bf16[2,128,8,128]{3,1,2,0:T(8,128)(2,1)} %get-tuple-element.207), channel_id=1, source_target_pairs={{0,16},{2,18},{4,20},{6,22},{8,24},{10,26},{12,28},{14,30},{1,17},... | collective-permute-start | bytes 1572872 | tf_op jit(solution)/shard_map/ppermute | solution.py:18
  204.6 106.1 %collective-permute-start.8 = (bf16[2,128,8,128]{3,1,2,0:T(8,128)(2,1)}, bf16[2,128,8,128]{3,1,2,0:T(8,128)(2,1)}, u32[]{:S(2)}, u32[]{:S(2)}) collective-permute-start(bf16[2,128,8,128]{3,1,2,0:T(8,128)(2,1)} %get-tuple-element.207), channel_id=1, source_target_pairs={{0,18},{2,20},{4,22},{6,24},{8,26},{10,28},{12,30},{1,19},{3,21},{... | collective-permute-start | bytes 1572872 | tf_op jit(solution)/shard_map/ppermute | solution.py:18
  264.5 63.2 %collective-permute-start.9 = (bf16[2,128,8,128]{3,1,2,0:T(8,128)(2,1)}, bf16[2,128,8,128]{3,1,2,0:T(8,128)(2,1)S(1)}, u32[]{:S(2)}, u32[]{:S(2)}) collective-permute-start(bf16[2,128,8,128]{3,1,2,0:T(8,128)(2,1)} %get-tuple-element.207), channel_id=1, source_target_pairs={{0,20},{2,22},{4,24},{6,26},{8,28},{10,30},{1,21},{3,23},{5,25},{7... | collective-permute-start | bytes 1572872 | tf_op jit(solution)/shard_map/ppermute | solution.py:18
  267.8 65.2 %collective-permute-start.10 = (bf16[2,128,8,128]{3,1,2,0:T(8,128)(2,1)}, bf16[2,128,8,128]{3,1,2,0:T(8,128)(2,1)S(1)}, u32[]{:S(2)}, u32[]{:S(2)}) collective-permute-start(bf16[2,128,8,128]{3,1,2,0:T(8,128)(2,1)} %get-tuple-element.207), channel_id=1, source_target_pairs={{0,22},{2,24},{4,26},{6,28},{8,30},{1,23},{3,25},{5,27},{7,29},{9,... | collective-permute-start | bytes 1572872 | tf_op jit(solution)/shard_map/ppermute | solution.py:18
  271.1 64.1 %collective-permute-start.11 = (bf16[2,128,8,128]{3,1,2,0:T(8,128)(2,1)}, bf16[2,128,8,128]{3,1,2,0:T(8,128)(2,1)S(1)}, u32[]{:S(2)}, u32[]{:S(2)}) collective-permute-start(bf16[2,128,8,128]{3,1,2,0:T(8,128)(2,1)} %get-tuple-element.207), channel_id=1, source_target_pairs={{0,24},{2,26},{4,28},{6,30},{1,25},{3,27},{5,29},{7,31}} | collective-permute-start | bytes 1572872 | tf_op jit(solution)/shard_map/ppermute | solution.py:18
  274.9 62.5 %collective-permute-start.12 = (bf16[2,128,8,128]{3,1,2,0:T(8,128)(2,1)}, bf16[2,128,8,128]{3,1,2,0:T(8,128)(2,1)S(1)}, u32[]{:S(2)}, u32[]{:S(2)}) collective-permute-start(bf16[2,128,8,128]{3,1,2,0:T(8,128)(2,1)} %get-tuple-element.207), channel_id=1, source_target_pairs={{0,26},{2,28},{4,30},{1,27},{3,29},{5,31}} | collective-permute-start | bytes 1572872 | tf_op jit(solution)/shard_map/ppermute | solution.py:18
  310.7 28.9 %collective-permute-start.13 = (bf16[2,128,8,128]{3,1,2,0:T(8,128)(2,1)}, bf16[2,128,8,128]{3,1,2,0:T(8,128)(2,1)S(1)}, u32[]{:S(2)}, u32[]{:S(2)}) collective-permute-start(bf16[2,128,8,128]{3,1,2,0:T(8,128)(2,1)} %get-tuple-element.207), channel_id=1, source_target_pairs={{0,28},{2,30},{1,29},{3,31}} | collective-permute-start | bytes 1572872 | tf_op jit(solution)/shard_map/ppermute | solution.py:18
  327.7 18.0 %collective-permute-start.14 = (bf16[2,128,8,128]{3,1,2,0:T(8,128)(2,1)}, bf16[2,128,8,128]{3,1,2,0:T(8,128)(2,1)S(1)}, u32[]{:S(2)}, u32[]{:S(2)}) collective-permute-start(bf16[2,128,8,128]{3,1,2,0:T(8,128)(2,1)} %get-tuple-element.207), channel_id=1, source_target_pairs={{0,30},{1,31}} | collective-permute-start | bytes 1572872 | tf_op jit(solution)/shard_map/ppermute | solution.py:18
  333.0 53.4 %collective-permute-start.23 = (bf16[2,128,8,128]{3,1,2,0:T(8,128)(2,1)S(1)}, bf16[2,128,8,128]{3,1,2,0:T(8,128)(2,1)}, u32[]{:S(2)}, u32[]{:S(2)}) collective-permute-start(bf16[2,128,8,128]{3,1,2,0:T(8,128)(2,1)S(1)} %copy-done.17), channel_id=1, source_target_pairs={{10,0},{12,2},{14,4},{16,6},{18,8},{20,10},{22,12},{24,14},{26,16}... | collective-permute-start | bytes 1572872 | tf_op jit(solution)/shard_map/ppermute | solution.py:18
  335.2 54.5 %collective-permute-start.24 = (bf16[2,128,8,128]{3,1,2,0:T(8,128)(2,1)S(1)}, bf16[2,128,8,128]{3,1,2,0:T(8,128)(2,1)}, u32[]{:S(2)}, u32[]{:S(2)}) collective-permute-start(bf16[2,128,8,128]{3,1,2,0:T(8,128)(2,1)S(1)} %copy-done.17), channel_id=1, source_target_pairs={{12,0},{14,2},{16,4},{18,6},{20,8},{22,10},{24,12},{26,14},{28,16}... | collective-permute-start | bytes 1572872 | tf_op jit(solution)/shard_map/ppermute | solution.py:18
  337.4 55.7 %collective-permute-start.25 = (bf16[2,128,8,128]{3,1,2,0:T(8,128)(2,1)S(1)}, bf16[2,128,8,128]{3,1,2,0:T(8,128)(2,1)S(1)}, u32[]{:S(2)}, u32[]{:S(2)}) collective-permute-start(bf16[2,128,8,128]{3,1,2,0:T(8,128)(2,1)S(1)} %copy-done.17), channel_id=1, source_target_pairs={{14,0},{16,2},{18,4},{20,6},{22,8},{24,10},{26,12},{28,14},{30,16}... | collective-permute-start | bytes 1572872 | tf_op jit(solution)/shard_map/ppermute | solution.py:18
  339.6 111.1 %collective-permute-start.26 = (bf16[2,128,8,128]{3,1,2,0:T(8,128)(2,1)S(1)}, bf16[2,128,8,128]{3,1,2,0:T(8,128)(2,1)}, u32[]{:S(2)}, u32[]{:S(2)}) collective-permute-start(bf16[2,128,8,128]{3,1,2,0:T(8,128)(2,1)S(1)} %copy-done.17), channel_id=1, source_target_pairs={{16,0},{18,2},{20,4},{22,6},{24,8},{26,10},{28,12},{30,14},{17,1},... | collective-permute-start | bytes 1572872 | tf_op jit(solution)/shard_map/ppermute | solution.py:18
  345.7 123.6 %collective-permute-start.27 = (bf16[2,128,8,128]{3,1,2,0:T(8,128)(2,1)S(1)}, bf16[2,128,8,128]{3,1,2,0:T(8,128)(2,1)}, u32[]{:S(2)}, u32[]{:S(2)}) collective-permute-start(bf16[2,128,8,128]{3,1,2,0:T(8,128)(2,1)S(1)} %copy-done.17), channel_id=1, source_target_pairs={{18,0},{20,2},{22,4},{24,6},{26,8},{28,10},{30,12},{19,1},{21,3},{... | collective-permute-start | bytes 1572872 | tf_op jit(solution)/shard_map/ppermute | solution.py:18
  386.4 86.8 %collective-permute-start.28 = (bf16[2,128,8,128]{3,1,2,0:T(8,128)(2,1)S(1)}, bf16[2,128,8,128]{3,1,2,0:T(8,128)(2,1)}, u32[]{:S(2)}, u32[]{:S(2)}) collective-permute-start(bf16[2,128,8,128]{3,1,2,0:T(8,128)(2,1)S(1)} %copy-done.17), channel_id=1, source_target_pairs={{20,0},{22,2},{24,4},{26,6},{28,8},{30,10},{21,1},{23,3},{25,5},{2... | collective-permute-start | bytes 1572872 | tf_op jit(solution)/shard_map/ppermute | solution.py:18
  389.7 105.2 %collective-permute-start.29 = (bf16[2,128,8,128]{3,1,2,0:T(8,128)(2,1)S(1)}, bf16[2,128,8,128]{3,1,2,0:T(8,128)(2,1)}, u32[]{:S(2)}, u32[]{:S(2)}) collective-permute-start(bf16[2,128,8,128]{3,1,2,0:T(8,128)(2,1)S(1)} %copy-done.17), channel_id=1, source_target_pairs={{22,0},{24,2},{26,4},{28,6},{30,8},{23,1},{25,3},{27,5},{29,7},{31... | collective-permute-start | bytes 1572872 | tf_op jit(solution)/shard_map/ppermute | solution.py:18
  393.1 105.0 %collective-permute-start.30 = (bf16[2,128,8,128]{3,1,2,0:T(8,128)(2,1)S(1)}, bf16[2,128,8,128]{3,1,2,0:T(8,128)(2,1)S(1)}, u32[]{:S(2)}, u32[]{:S(2)}) collective-permute-start(bf16[2,128,8,128]{3,1,2,0:T(8,128)(2,1)S(1)} %copy-done.17), channel_id=1, source_target_pairs={{24,0},{26,2},{28,4},{30,6},{25,1},{27,3},{29,5},{31,7}} | collective-permute-start | bytes 1572872 | tf_op jit(solution)/shard_map/ppermute | solution.py:18
  450.7 49.8 %collective-permute-start.31 = (bf16[2,128,8,128]{3,1,2,0:T(8,128)(2,1)S(1)}, bf16[2,128,8,128]{3,1,2,0:T(8,128)(2,1)S(1)}, u32[]{:S(2)}, u32[]{:S(2)}) collective-permute-start(bf16[2,128,8,128]{3,1,2,0:T(8,128)(2,1)S(1)} %copy-done.17), channel_id=1, source_target_pairs={{26,0},{28,2},{30,4},{27,1},{29,3},{31,5}} | collective-permute-start | bytes 1572872 | tf_op jit(solution)/shard_map/ppermute | solution.py:18
  469.3 33.4 %collective-permute-start.32 = (bf16[2,128,8,128]{3,1,2,0:T(8,128)(2,1)S(1)}, bf16[2,128,8,128]{3,1,2,0:T(8,128)(2,1)S(1)}, u32[]{:S(2)}, u32[]{:S(2)}) collective-permute-start(bf16[2,128,8,128]{3,1,2,0:T(8,128)(2,1)S(1)} %copy-done.17), channel_id=1, source_target_pairs={{28,0},{30,2},{29,1},{31,3}} | collective-permute-start | bytes 1572872 | tf_op jit(solution)/shard_map/ppermute | solution.py:18
  473.2 31.7 %collective-permute-start.33 = (bf16[2,128,8,128]{3,1,2,0:T(8,128)(2,1)S(1)}, bf16[2,128,8,128]{3,1,2,0:T(8,128)(2,1)}, u32[]{:S(2)}, u32[]{:S(2)}) collective-permute-start(bf16[2,128,8,128]{3,1,2,0:T(8,128)(2,1)S(1)} %copy-done.17), channel_id=1, source_target_pairs={{30,0},{31,1}} | collective-permute-start | bytes 1572872 | tf_op jit(solution)/shard_map/ppermute | solution.py:18
  494.8 19.4 %collective-permute-start.19 = (f32[3,8,256]{2,1,0:T(8,128)}, f32[3,8,256]{2,1,0:T(8,128)S(1)}, u32[]{:S(2)}, u32[]{:S(2)}) collective-permute-start(f32[3,8,256]{2,1,0:T(8,128)} %get-tuple-element.152), channel_id=1, source_target_pairs={{2,0},{4,2},{6,4},{8,6},{10,8},{12,10},{14,12},{16,14},{18,16},{20... | collective-permute-start | bytes 73736 | tf_op jit(solution)/shard_map/ppermute | solution.py:18
  498.1 16.7 %collective-permute-start.20 = (f32[3,8,256]{2,1,0:T(8,128)}, f32[3,8,256]{2,1,0:T(8,128)S(1)}, u32[]{:S(2)}, u32[]{:S(2)}) collective-permute-start(f32[3,8,256]{2,1,0:T(8,128)} %get-tuple-element.152), channel_id=1, source_target_pairs={{4,0},{6,2},{8,4},{10,6},{12,8},{14,10},{16,12},{18,14},{20,16},{2... | collective-permute-start | bytes 73736 | tf_op jit(solution)/shard_map/ppermute | solution.py:18
  500.5 15.2 %collective-permute-start.21 = (f32[3,8,256]{2,1,0:T(8,128)}, f32[3,8,256]{2,1,0:T(8,128)S(1)}, u32[]{:S(2)}, u32[]{:S(2)}) collective-permute-start(f32[3,8,256]{2,1,0:T(8,128)} %get-tuple-element.152), channel_id=1, source_target_pairs={{6,0},{8,2},{10,4},{12,6},{14,8},{16,10},{18,12},{20,14},{22,16},{... | collective-permute-start | bytes 73736 | tf_op jit(solution)/shard_map/ppermute | solution.py:18
  502.7 14.2 %collective-permute-start.22 = (f32[3,8,256]{2,1,0:T(8,128)}, f32[3,8,256]{2,1,0:T(8,128)S(1)}, u32[]{:S(2)}, u32[]{:S(2)}) collective-permute-start(f32[3,8,256]{2,1,0:T(8,128)} %get-tuple-element.152), channel_id=1, source_target_pairs={{8,0},{10,2},{12,4},{14,6},{16,8},{18,10},{20,12},{22,14},{24,16},... | collective-permute-start | bytes 73736 | tf_op jit(solution)/shard_map/ppermute | solution.py:18
  518.6 25.2 %collective-permute-start.34 = (f32[3,8,128]{1,2,0:T(8,128)S(1)}, f32[3,8,128]{1,2,0:T(8,128)S(1)}, u32[]{:S(2)}, u32[]{:S(2)}) collective-permute-start(f32[3,8,128]{1,2,0:T(8,128)S(1)} %get-tuple-element.197), channel_id=1, source_target_pairs={{10,0},{12,2},{14,4},{16,6},{18,8},{20,10},{22,12},{24,14},{26,16}... | collective-permute-start | bytes 36872 | tf_op jit(solution)/shard_map/ppermute | solution.py:18
  519.9 25.2 %collective-permute-start.35 = (f32[3,8,128]{1,2,0:T(8,128)S(1)}, f32[3,8,128]{1,2,0:T(8,128)S(1)}, u32[]{:S(2)}, u32[]{:S(2)}) collective-permute-start(f32[3,8,128]{1,2,0:T(8,128)S(1)} %get-tuple-element.197), channel_id=1, source_target_pairs={{12,0},{14,2},{16,4},{18,6},{20,8},{22,10},{24,12},{26,14},{28,16}... | collective-permute-start | bytes 36872 | tf_op jit(solution)/shard_map/ppermute | solution.py:18
  521.2 25.3 %collective-permute-start.36 = (f32[3,8,128]{1,2,0:T(8,128)S(1)}, f32[3,8,128]{1,2,0:T(8,128)S(1)}, u32[]{:S(2)}, u32[]{:S(2)}) collective-permute-start(f32[3,8,128]{1,2,0:T(8,128)S(1)} %get-tuple-element.197), channel_id=1, source_target_pairs={{14,0},{16,2},{18,4},{20,6},{22,8},{24,10},{26,12},{28,14},{30,16}... | collective-permute-start | bytes 36872 | tf_op jit(solution)/shard_map/ppermute | solution.py:18
  522.5 52.0 %collective-permute-start.37 = (f32[3,8,128]{1,2,0:T(8,128)S(1)}, f32[3,8,128]{1,2,0:T(8,128)S(1)}, u32[]{:S(2)}, u32[]{:S(2)}) collective-permute-start(f32[3,8,128]{1,2,0:T(8,128)S(1)} %get-tuple-element.197), channel_id=1, source_target_pairs={{16,0},{18,2},{20,4},{22,6},{24,8},{26,10},{28,12},{30,14},{17,1},... | collective-permute-start | bytes 36872 | tf_op jit(solution)/shard_map/ppermute | solution.py:18
  523.9 52.6 %collective-permute-start.38 = (f32[3,8,128]{1,2,0:T(8,128)S(1)}, f32[3,8,128]{1,2,0:T(8,128)S(1)}, u32[]{:S(2)}, u32[]{:S(2)}) collective-permute-start(f32[3,8,128]{1,2,0:T(8,128)S(1)} %get-tuple-element.197), channel_id=1, source_target_pairs={{18,0},{20,2},{22,4},{24,6},{26,8},{28,10},{30,12},{19,1},{21,3},{... | collective-permute-start | bytes 36872 | tf_op jit(solution)/shard_map/ppermute | solution.py:18
  543.8 34.1 %collective-permute-start.39 = (f32[3,8,128]{1,2,0:T(8,128)S(1)}, f32[3,8,128]{1,2,0:T(8,128)S(1)}, u32[]{:S(2)}, u32[]{:S(2)}) collective-permute-start(f32[3,8,128]{1,2,0:T(8,128)S(1)} %get-tuple-element.197), channel_id=1, source_target_pairs={{20,0},{22,2},{24,4},{26,6},{28,8},{30,10},{21,1},{23,3},{25,5},{2... | collective-permute-start | bytes 36872 | tf_op jit(solution)/shard_map/ppermute | solution.py:18
  545.2 34.1 %collective-permute-start.40 = (f32[3,8,128]{1,2,0:T(8,128)S(1)}, f32[3,8,128]{1,2,0:T(8,128)S(1)}, u32[]{:S(2)}, u32[]{:S(2)}) collective-permute-start(f32[3,8,128]{1,2,0:T(8,128)S(1)} %get-tuple-element.197), channel_id=1, source_target_pairs={{22,0},{24,2},{26,4},{28,6},{30,8},{23,1},{25,3},{27,5},{29,7},{31... | collective-permute-start | bytes 36872 | tf_op jit(solution)/shard_map/ppermute | solution.py:18
  546.6 32.8 %collective-permute-start.41 = (f32[3,8,128]{1,2,0:T(8,128)S(1)}, f32[3,8,128]{1,2,0:T(8,128)S(1)}, u32[]{:S(2)}, u32[]{:S(2)}) collective-permute-start(f32[3,8,128]{1,2,0:T(8,128)S(1)} %get-tuple-element.197), channel_id=1, source_target_pairs={{24,0},{26,2},{28,4},{30,6},{25,1},{27,3},{29,5},{31,7}} | collective-permute-start | bytes 36872 | tf_op jit(solution)/shard_map/ppermute | solution.py:18
  574.5 8.8 %collective-permute-start.42 = (f32[3,8,128]{1,2,0:T(8,128)S(1)}, f32[3,8,128]{1,2,0:T(8,128)S(1)}, u32[]{:S(2)}, u32[]{:S(2)}) collective-permute-start(f32[3,8,128]{1,2,0:T(8,128)S(1)} %get-tuple-element.197), channel_id=1, source_target_pairs={{26,0},{28,2},{30,4},{27,1},{29,3},{31,5}} | collective-permute-start | bytes 36872 | tf_op jit(solution)/shard_map/ppermute | solution.py:18
  576.5 13.8 %collective-permute-start.43 = (f32[3,8,128]{1,2,0:T(8,128)S(1)}, f32[3,8,128]{1,2,0:T(8,128)S(1)}, u32[]{:S(2)}, u32[]{:S(2)}) collective-permute-start(f32[3,8,128]{1,2,0:T(8,128)S(1)} %get-tuple-element.197), channel_id=1, source_target_pairs={{28,0},{30,2},{29,1},{31,3}} | collective-permute-start | bytes 36872 | tf_op jit(solution)/shard_map/ppermute | solution.py:18
  577.9 12.9 %collective-permute-start.44 = (f32[3,8,128]{1,2,0:T(8,128)S(1)}, f32[3,8,128]{1,2,0:T(8,128)S(1)}, u32[]{:S(2)}, u32[]{:S(2)}) collective-permute-start(f32[3,8,128]{1,2,0:T(8,128)S(1)} %get-tuple-element.197), channel_id=1, source_target_pairs={{30,0},{31,1}} | collective-permute-start | bytes 36872 | tf_op jit(solution)/shard_map/ppermute | solution.py:18
  (113 other events, 4930.1 us)
Sparse Core Ops, SparseCore 0:
  9.6 59.4 all-gather.1
